TPU v7x, 32 devices: a whole 2x2x4 slice. The times are simulated.
32 devices in a mesh: seq: 8 (over z, x), kvh: 4 (over y, core).
Axes of the slice: x: 2, y: 2, z: 4, core: 2. Of those that a mesh axis runs over, the one named last changes fastest.
Arguments:
- queries: bfloat16 [2048, 16384], P(('seq', 'kvh')), may hold values from -48 to 48
- key_rows: bfloat16 [2048, 1024], P(('seq', 'kvh')), may hold values from -6 to 6
- value_rows: bfloat16 [2048, 1024], P(('seq', 'kvh')), may hold values from -6 to 6
- doc_lengths: int32 [8], replicated, may hold values from 1 to 512, 2048 in all
Outputs:
- attended: bfloat16 [2048, 16384], P(('seq', 'kvh'))
Inputs may be any that keep to these rules, and one draw needn't show every extreme that they name: `doc_lengths`: the lengths add up to 2048; the longest document has exactly 512 tokens.
All inputs are finite; a program needn't handle non-finite values.
Results may differ from a plain program's by a relative error of at most 0.004.
Values may be sent and summed in bfloat16 or wider, within the bound.
No kernel may reach another device: no remote copies, remote signals or barrier semaphores. Data moves between devices by JAX's collectives and lax.ppermute only.
A program may use at most 64 MiB of HBM per device.

v0:
```python
import math

import jax
import jax.numpy as jnp
from jax import lax
from jax.sharding import PartitionSpec as P

DH = 128


def shifted(block, axis, distance):
    devices = range(lax.axis_size(axis))
    route = [(i - distance, i) for i in devices if i - distance in devices]
    return lax.ppermute(block, axis, route)


def doc_start(position, doc_ends, doc_lengths):
    return jnp.sum(
        jnp.where(doc_ends[None, :] <= position[:, None], doc_lengths[None, :], 0), axis=1
    )


def absorb(running, query_side, key_tile, key_pos, kv_feat, kv_heads):
    query_block, row_pos, row_start, lowest, highest = query_side

    def compute(current):
        top_old, total_old, acc_old = current
        tile_rows = key_tile.shape[0]
        key_part = key_tile[:, :kv_feat].reshape(tile_rows, kv_heads, DH).transpose(1, 0, 2)
        value_part = key_tile[:, kv_feat:].reshape(tile_rows, kv_heads, DH).transpose(1, 0, 2)
        scores = jnp.einsum(
            "hqd,hkd->hqk", query_block, key_part, preferred_element_type=jnp.float32
        ) * (1.0 / math.sqrt(DH))
        allowed = (key_pos[None, :] <= row_pos[:, None]) & (key_pos[None, :] >= row_start[:, None])
        scores = jnp.where(allowed[None], scores, -jnp.inf)
        top_new = jnp.maximum(top_old, jnp.max(scores, axis=2))
        anchor = jnp.where(jnp.isfinite(top_new), top_new, 0.0)
        weights = jnp.exp(scores - anchor[:, :, None])
        shrink = jnp.exp(top_old - anchor)
        total_new = total_old * shrink + jnp.sum(weights, axis=2)
        acc_new = acc_old * shrink[:, :, None] + jnp.einsum(
            "hqk,hkd->hqd",
            weights.astype(jnp.bfloat16),
            value_part,
            preferred_element_type=jnp.float32,
        )
        return (top_new, total_new, acc_new)

    touched = jnp.any((key_pos >= lowest) & (key_pos <= highest))
    return lax.cond(touched, compute, lambda current: current, running)


def on_device(queries, key_rows, value_rows, doc_lengths):
    shards = lax.axis_size("seq")
    my_shard = lax.axis_index("seq")
    head_queries, head_keys, head_values = (
        lax.all_to_all(queries, "kvh", split_axis=1, concat_axis=0, tiled=True),
        lax.all_to_all(key_rows, "kvh", split_axis=1, concat_axis=0, tiled=True),
        lax.all_to_all(value_rows, "kvh", split_axis=1, concat_axis=0, tiled=True),
    )
    dev_rows = head_queries.shape[0]
    half_rows = dev_rows // 2
    kv_feat = head_keys.shape[1]
    kv_heads = kv_feat // DH
    group_size = head_queries.shape[1] // kv_feat
    kv_slab = jnp.concatenate([head_keys, head_values], axis=1)
    seq_total = dev_rows * shards
    longest = min(13 * half_rows, seq_total // 4)
    lookback = (longest + half_rows - 2) // half_rows
    reach_dev = min(lookback, shards - 1)
    doc_ends = jnp.cumsum(doc_lengths)
    query_sides = []
    block_ids = []
    for side_no in range(2):
        block_id = my_shard if side_no == 0 else 2 * shards - 1 - my_shard
        position = block_id * half_rows + jnp.arange(half_rows, dtype=jnp.int32)
        starts = doc_start(position, doc_ends, doc_lengths)
        q_block = head_queries[side_no * half_rows : (side_no + 1) * half_rows]
        q_block = (
            q_block.reshape(half_rows, kv_heads, group_size, DH)
            .transpose(1, 0, 2, 3)
            .reshape(kv_heads, half_rows * group_size, DH)
        )
        query_sides.append(
            (
                q_block,
                jnp.repeat(position, group_size),
                jnp.repeat(starts, group_size),
                starts[0],
                position[-1],
            )
        )
        block_ids.append(block_id)
    initial = (
        jnp.full((kv_heads, half_rows * group_size), -jnp.inf, jnp.float32),
        jnp.zeros((kv_heads, half_rows * group_size), jnp.float32),
        jnp.zeros((kv_heads, half_rows * group_size, DH), jnp.float32),
    )
    tile_count = (lookback + 2) // 2
    offsets = jnp.arange(half_rows, dtype=jnp.int32)

    def run_tiles(fetch_side):
        results = []
        for side_no in range(2):

            def visit_tile(tile_no, running, side_no=side_no):
                early_rows, early_pos = fetch_side(side_no, 2 * tile_no + 1)
                late_rows, late_pos = fetch_side(side_no, 2 * tile_no)
                key_tile = jnp.concatenate([early_rows, late_rows], axis=0)
                key_pos = jnp.concatenate([early_pos, late_pos])
                return absorb(running, query_sides[side_no], key_tile, key_pos, kv_feat, kv_heads)

            results.append(lax.fori_loop(0, tile_count, visit_tile, initial))
        return results

    lower = jnp.zeros((reach_dev + 1,) + kv_slab.shape, kv_slab.dtype).at[0].set(kv_slab)
    upper = jnp.zeros((reach_dev + 1,) + kv_slab.shape, kv_slab.dtype).at[0].set(kv_slab)

    def walk(hop_no, carried):
        down_piece, up_piece, lower_buf, upper_buf = carried
        down_piece = shifted(down_piece, "seq", 1)
        up_piece = shifted(up_piece, "seq", -1)
        lower_buf = lax.dynamic_update_index_in_dim(lower_buf, down_piece, hop_no, 0)
        upper_buf = lax.dynamic_update_index_in_dim(upper_buf, up_piece, hop_no, 0)
        return (down_piece, up_piece, lower_buf, upper_buf)

    walked = lax.fori_loop(1, reach_dev + 1, walk, (kv_slab, kv_slab, lower, upper))
    lower = walked[2]
    upper = walked[3]
    window = jnp.concatenate([lower[::-1], upper[1:]], axis=0)

    def fetch_whole(side_no, back):
        wanted = block_ids[side_no] - back
        valid = (wanted >= 0) & (back <= lookback)
        holder = jnp.where(wanted < shards, wanted, 2 * shards - 1 - wanted)
        half_no = jnp.where(wanted < shards, 0, 1)
        slot = jnp.clip(holder - my_shard + reach_dev, 0, 2 * reach_dev)
        rows_in = lax.dynamic_slice(
            window, (slot, half_no * half_rows, 0), (1, half_rows, window.shape[2])
        )[0]
        return (rows_in, jnp.where(valid, wanted * half_rows + offsets, -1))

    finals = run_tiles(fetch_whole)
    outputs = []
    for side_no in range(2):
        acc_rows = finals[side_no][2]
        total_rows = finals[side_no][1]
        normed = acc_rows / total_rows[:, :, None]
        normed = (
            normed.reshape(kv_heads, half_rows, group_size, DH)
            .transpose(1, 0, 2, 3)
            .reshape(half_rows, kv_heads * group_size * DH)
        )
        outputs.append(normed.astype(jnp.bfloat16))
    merged = jnp.concatenate(outputs, axis=0)
    return lax.all_to_all(merged, "kvh", split_axis=0, concat_axis=1, tiled=True)


def solution(mesh):
    return jax.shard_map(
        on_device,
        mesh=mesh,
        in_specs=(P(("seq", "kvh"), None), P(("seq", "kvh"), None), P(("seq", "kvh"), None), P()),
        out_specs=P(("seq", "kvh"), None),
        check_vma=False,
    )
```

profile of v0, /device:TPU:8, one launch (start us, length us, event | category | flops | bytes accessed | tf_op | source)
XLA Modules:
  0.0 202.7 jit_solution(5594073410735844283)
XLA Ops:
  0.0 1.6 copy.67
  1.6 3.3 %all-to-all-start.1 = ((bf16[64,4,256]{2,0,1:T(8,128)(2,1)}), bf16[64,4,256]{2,0,1:T(8,128)(2,1)S(1)}, u32[]{:S(2)}, u32[]{:S(2)}) async-start(bf16[64,4,256]{2,0,1:T(8,128)(2,1)} %bitcast.85), calls=%async_computation.1 | async-start | bytes 262144 | tf_op jit(solution)/shard_map/all_to_all | solution.py:59
  6.3 1.6 copy.68
  7.9 3.1 %copy.66 = bf16[8,4,8,4096]{3,2,0,1:T(8,128)(2,1)} copy(bf16[8,4,8,4096]{3,2,1,0:T(8,128)(2,1)} %bitcast.113) | data formatting | bytes 4194304 | tf_op jit(solution)/shard_map/all_to_all | solution.py:57
  11.7 3.3 %all-to-all-start = ((bf16[64,4,256]{2,0,1:T(8,128)(2,1)}), bf16[64,4,256]{2,0,1:T(8,128)(2,1)S(1)}, u32[]{:S(2)}, u32[]{:S(2)}) async-start(bf16[64,4,256]{2,0,1:T(8,128)(2,1)} %bitcast.86), calls=%async_computation | async-start | bytes 262144 | tf_op jit(solution)/shard_map/all_to_all | solution.py:58
  15.2 4.5 %all-to-all-done = bf16[64,4,256]{2,0,1:T(8,128)(2,1)S(1)} async-done(((bf16[64,4,256]{2,0,1:T(8,128)(2,1)}), bf16[64,4,256]{2,0,1:T(8,128)(2,1)S(1)}, u32[]{:S(2)}, u32[]{:S(2)}) %all-to-all-start) | async-done | bytes 131104 | tf_op jit(solution)/shard_map/all_to_all | solution.py:58
  19.7 4.4 %all-to-all-start.2 = ((bf16[64,4,4096]{2,0,1:T(8,128)(2,1)}), bf16[64,4,4096]{2,0,1:T(8,128)(2,1)}, u32[]{:S(2)}, u32[]{:S(2)}) async-start(bf16[64,4,4096]{2,0,1:T(8,128)(2,1)} %bitcast.84), calls=%async_computation.2 | async-start | bytes 4194304 | tf_op jit(solution)/shard_map/all_to_all | solution.py:57
  25.1 70.2 %while.59 = (s32[]{:T(128)}, bf16[256,512]{1,0:T(8,128)(2,1)S(1)}, bf16[256,512]{1,0:T(8,128)(2,1)}, bf16[5,256,512]{2,1,0:T(8,128)(2,1)S(1)}, bf16[5,256,512]{2...) while((s32[]{:T(128)}, bf16[256,512]{1,0:T(8,128)(2,1)S(1)}, bf16[256,512]{1,0:T(8,128)(2,1)}, ...), condition=%wide.region_1.2_spmd, body=%wide.region_0.0_spmd.sunk | while | flops 5 | bytes 4194519 | solution.py:127
  25.1 3.4 %collective-permute-start = (bf16[256,512]{1,0:T(8,128)(2,1)S(1)}, bf16[256,512]{1,0:T(8,128)(2,1)S(1)}, u32[]{:S(2)}, u32[]{:S(2)}) collective-permute-start(bf16[256,512]{1,0:T(8,128)(2,1)S(1)} %get-tuple-element.1065), channel_id=1, source_target_pairs={{0,4},{4,8},{8,12},{12,16},{16,20},{20,24},{24,28},{1,5},{5,9},{9,... | collective-permute-start | bytes 786440 | tf_op jit(solution)/shard_map/while/body/eval_jaxpr/ppermute | solution.py:14
  28.5 3.3 %collective-permute-start.1 = (bf16[256,512]{1,0:T(8,128)(2,1)}, bf16[256,512]{1,0:T(8,128)(2,1)S(1)}, u32[]{:S(2)}, u32[]{:S(2)}) collective-permute-start(bf16[256,512]{1,0:T(8,128)(2,1)} %get-tuple-element.1066), channel_id=1, source_target_pairs={{4,0},{8,4},{12,8},{16,12},{20,16},{24,20},{28,24},{5,1},{9,5},{13... | collective-permute-start | bytes 786440 | tf_op jit(solution)/shard_map/while/body/eval_jaxpr/ppermute | solution.py:14
  31.9 8.4 %collective-permute-done = bf16[256,512]{1,0:T(8,128)(2,1)S(1)} collective-permute-done((bf16[256,512]{1,0:T(8,128)(2,1)S(1)}, bf16[256,512]{1,0:T(8,128)(2,1)S(1)}, u32[]{:S(2)}, u32[]{:S(2)}) %collective-permute-start) | collective-permute-done | bytes 262176 | tf_op jit(solution)/shard_map/while/body/eval_jaxpr/ppermute | solution.py:14
  40.3 1.9 collective-permute-done.1
  42.9 2.5 %collective-permute-start = (bf16[256,512]{1,0:T(8,128)(2,1)S(1)}, bf16[256,512]{1,0:T(8,128)(2,1)S(1)}, u32[]{:S(2)}, u32[]{:S(2)}) collective-permute-start(bf16[256,512]{1,0:T(8,128)(2,1)S(1)} %get-tuple-element.1065), channel_id=1, source_target_pairs={{0,4},{4,8},{8,12},{12,16},{16,20},{20,24},{24,28},{1,5},{5,9},{9,... | collective-permute-start | bytes 786440 | tf_op jit(solution)/shard_map/while/body/eval_jaxpr/ppermute | solution.py:14
  45.5 4.2 %collective-permute-start.1 = (bf16[256,512]{1,0:T(8,128)(2,1)}, bf16[256,512]{1,0:T(8,128)(2,1)S(1)}, u32[]{:S(2)}, u32[]{:S(2)}) collective-permute-start(bf16[256,512]{1,0:T(8,128)(2,1)} %get-tuple-element.1066), channel_id=1, source_target_pairs={{4,0},{8,4},{12,8},{16,12},{20,16},{24,20},{28,24},{5,1},{9,5},{13... | collective-permute-start | bytes 786440 | tf_op jit(solution)/shard_map/while/body/eval_jaxpr/ppermute | solution.py:14
  49.7 4.5 %collective-permute-done = bf16[256,512]{1,0:T(8,128)(2,1)S(1)} collective-permute-done((bf16[256,512]{1,0:T(8,128)(2,1)S(1)}, bf16[256,512]{1,0:T(8,128)(2,1)S(1)}, u32[]{:S(2)}, u32[]{:S(2)}) %collective-permute-start) | collective-permute-done | bytes 262176 | tf_op jit(solution)/shard_map/while/body/eval_jaxpr/ppermute | solution.py:14
  54.2 5.5 %collective-permute-done.1 = bf16[256,512]{1,0:T(8,128)(2,1)S(1)} collective-permute-done((bf16[256,512]{1,0:T(8,128)(2,1)}, bf16[256,512]{1,0:T(8,128)(2,1)S(1)}, u32[]{:S(2)}, u32[]{:S(2)}) %collective-permute-start.1) | collective-permute-done | bytes 262176 | tf_op jit(solution)/shard_map/while/body/eval_jaxpr/ppermute | solution.py:14
  60.5 1.9 collective-permute-start
  62.4 4.8 %collective-permute-start.1 = (bf16[256,512]{1,0:T(8,128)(2,1)}, bf16[256,512]{1,0:T(8,128)(2,1)S(1)}, u32[]{:S(2)}, u32[]{:S(2)}) collective-permute-start(bf16[256,512]{1,0:T(8,128)(2,1)} %get-tuple-element.1066), channel_id=1, source_target_pairs={{4,0},{8,4},{12,8},{16,12},{20,16},{24,20},{28,24},{5,1},{9,5},{13... | collective-permute-start | bytes 786440 | tf_op jit(solution)/shard_map/while/body/eval_jaxpr/ppermute | solution.py:14
  67.2 4.4 %collective-permute-done = bf16[256,512]{1,0:T(8,128)(2,1)S(1)} collective-permute-done((bf16[256,512]{1,0:T(8,128)(2,1)S(1)}, bf16[256,512]{1,0:T(8,128)(2,1)S(1)}, u32[]{:S(2)}, u32[]{:S(2)}) %collective-permute-start) | collective-permute-done | bytes 262176 | tf_op jit(solution)/shard_map/while/body/eval_jaxpr/ppermute | solution.py:14
  71.6 5.5 %collective-permute-done.1 = bf16[256,512]{1,0:T(8,128)(2,1)S(1)} collective-permute-done((bf16[256,512]{1,0:T(8,128)(2,1)}, bf16[256,512]{1,0:T(8,128)(2,1)S(1)}, u32[]{:S(2)}, u32[]{:S(2)}) %collective-permute-start.1) | collective-permute-done | bytes 262176 | tf_op jit(solution)/shard_map/while/body/eval_jaxpr/ppermute | solution.py:14
  77.9 1.9 collective-permute-start
  79.8 4.8 %collective-permute-start.1 = (bf16[256,512]{1,0:T(8,128)(2,1)}, bf16[256,512]{1,0:T(8,128)(2,1)S(1)}, u32[]{:S(2)}, u32[]{:S(2)}) collective-permute-start(bf16[256,512]{1,0:T(8,128)(2,1)} %get-tuple-element.1066), channel_id=1, source_target_pairs={{4,0},{8,4},{12,8},{16,12},{20,16},{24,20},{28,24},{5,1},{9,5},{13... | collective-permute-start | bytes 786440 | tf_op jit(solution)/shard_map/while/body/eval_jaxpr/ppermute | solution.py:14
  84.7 4.4 %collective-permute-done = bf16[256,512]{1,0:T(8,128)(2,1)S(1)} collective-permute-done((bf16[256,512]{1,0:T(8,128)(2,1)S(1)}, bf16[256,512]{1,0:T(8,128)(2,1)S(1)}, u32[]{:S(2)}, u32[]{:S(2)}) %collective-permute-start) | collective-permute-done | bytes 262176 | tf_op jit(solution)/shard_map/while/body/eval_jaxpr/ppermute | solution.py:14
  89.0 5.5 %collective-permute-done.1 = bf16[256,512]{1,0:T(8,128)(2,1)S(1)} collective-permute-done((bf16[256,512]{1,0:T(8,128)(2,1)}, bf16[256,512]{1,0:T(8,128)(2,1)S(1)}, u32[]{:S(2)}, u32[]{:S(2)}) %collective-permute-start.1) | collective-permute-done | bytes 262176 | tf_op jit(solution)/shard_map/while/body/eval_jaxpr/ppermute | solution.py:14
  95.3 1.5 copy.47
  96.8 2.2 %slice.72 = bf16[4,256,512]{1,2,0:T(8,128)(2,1)} slice(bf16[5,256,512]{1,2,0:T(8,128)(2,1)} %copy.47), slice={[1:5], [0:256], [0:512]} | slice | bytes 2097152 | tf_op jit(solution)/shard_map/slice | solution.py:130
  99.7 2.9 %pad_maximum_fusion.2 = bf16[9,256,512]{1,2,0:T(8,128)(2,1)} fusion(bf16[4,256,512]{1,2,0:T(8,128)(2,1)} %slice.72, bf16[5,256,512]{1,2,0:T(8,128)(2,1)S(1)} %rev.3), kind=kLoop, calls=%fused_computation.64 | loop fusion | flops 1179648 | bytes 4718592 | tf_op jit(solution)/shard_map/concatenate | solution.py:130
  102.6 2.7 %fusion.41 = (bf16[2,64,4096]{2,1,0:T(8,128)(2,1)}, bf16[2,64,4096]{2,1,0:T(8,128)(2,1)S(1)}) fusion(bf16[4,64,4096]{2,1,0:T(8,128)(2,1)} %bitcast.19), kind=kLoop, calls=%fused_computation.79 | loop fusion | bytes 4194304 | tf_op jit(solution)/shard_map/slice | solution.py:78
  105.5 1.1 copy.51
  106.8 35.8 %while.61 = (s32[]{:T(128)}, f32[2,2048]{1,0:T(2,128)S(1)}, f32[2,2048]{1,0:T(2,128)S(1)}, f32[2,2048,128]{2,1,0:T(8,128)S(1)}, s32[]{:T(128)}, /*index=5*/s32[]...) while((s32[]{:T(128)}, f32[2,2048]{1,0:T(2,128)S(1)}, ...), condition=%wide.region_18.19_spmd.clone.clone, body=%wide.region_12.18_spmd.clone.clone.sunk | while | flops 551577664 | bytes 39410436 | solution.py:113
  106.9 1.3 and_reduce_fusion.5
  108.9 1.0 dynamic-slice_bitcast_fusion.7
  109.9 8.8 %conditional.9 = ((f32[2,2048]{1,0:T(2,128)S(1)}, f32[2,2048]{1,0:T(2,128)S(1)}, f32[2,2048,128]{2,1,0:T(8,128)S(1)})) conditional(s32[]{:T(128)} %convert_element_type.65, (f32[2,2048]{1,0:T(2,128)S(1)}, f32[2,2048]{1,0:T(2,128)S(1)}, f32[2,2048,128]{2,1,0:T(8,128)S(1)}) %tuple.145, (s32[256]{0:T(256)S(1)}, s32[128]{0:T(128)S(1)}, ...), branch_computations={%region_14.14_spmd, %region_15.17_spmd} | conditional | flops 551051264 | bytes 38357052 | solution.py:50
  110.9 2.2 %fusion.25 = (f32[2,2048]{1,0:T(2,128)S(1)}, f32[2,2048,256]{1,2,0:T(8,128)S(1)}) fusion(pred[2048,256]{0,1:T(8,128)(4,1)S(1)} %compare_and_fusion.1, bf16[2,2048,128]{2,1,0:T(8,128)(2,1)} %get-tuple-element.591, bf16[256,2,128]{2,0,1:T(8,128)(2,1)S(1)} %copy.41), kind=kOutput, calls=%fused_computation.29 | convolution fusion | flops 271577088 | bytes 5914624 | tf_op jit(solution)/shard_map/while/body/eval_jaxpr/cond/branch_1_fun/hqd,hkd->hqk/dot_general | solution.py:31
  113.1 1.0 fusion.27
  115.2 3.5 %convolution_add_fusion.1 = f32[2,2048,128]{2,1,0:T(8,128)S(1)} fusion(f32[2,2048,256]{1,2,0:T(8,128)} %copy-done, f32[2,2048,128]{2,1,0:T(8,128)S(1)} %get-tuple-element.594, f32[2,2048]{1,0:T(2,128)S(1)} %get-tuple-element.821, pred[2048,256]{0,1:T(8,128)(4,1)S(1)} %compare_and_fusion.1, f32[2,2048]{1,0:T(2,128)S(1)} %get-tuple-element.820, ...), kind=kOutput, calls=%fused_computation.32 | convolution fusion | flops 273678336 | bytes 9076736 | tf_op jit(solution)/shard_map/while/body/eval_jaxpr/cond/branch_1_fun/hqk,hkd->hqd/dot_general | solution.py:41
  118.8 1.3 and_reduce_fusion.5
  120.8 1.0 dynamic-slice_bitcast_fusion.7
  121.8 8.8 %conditional.9 = ((f32[2,2048]{1,0:T(2,128)S(1)}, f32[2,2048]{1,0:T(2,128)S(1)}, f32[2,2048,128]{2,1,0:T(8,128)S(1)})) conditional(s32[]{:T(128)} %convert_element_type.65, (f32[2,2048]{1,0:T(2,128)S(1)}, f32[2,2048]{1,0:T(2,128)S(1)}, f32[2,2048,128]{2,1,0:T(8,128)S(1)}) %tuple.145, (s32[256]{0:T(256)S(1)}, s32[128]{0:T(128)S(1)}, ...), branch_computations={%region_14.14_spmd, %region_15.17_spmd} | conditional | flops 551051264 | bytes 38357052 | solution.py:50
  122.8 2.2 %fusion.25 = (f32[2,2048]{1,0:T(2,128)S(1)}, f32[2,2048,256]{1,2,0:T(8,128)S(1)}) fusion(pred[2048,256]{0,1:T(8,128)(4,1)S(1)} %compare_and_fusion.1, bf16[2,2048,128]{2,1,0:T(8,128)(2,1)} %get-tuple-element.591, bf16[256,2,128]{2,0,1:T(8,128)(2,1)S(1)} %copy.41), kind=kOutput, calls=%fused_computation.29 | convolution fusion | flops 271577088 | bytes 5914624 | tf_op jit(solution)/shard_map/while/body/eval_jaxpr/cond/branch_1_fun/hqd,hkd->hqk/dot_general | solution.py:31
  127.1 3.5 %convolution_add_fusion.1 = f32[2,2048,128]{2,1,0:T(8,128)S(1)} fusion(f32[2,2048,256]{1,2,0:T(8,128)} %copy-done, f32[2,2048,128]{2,1,0:T(8,128)S(1)} %get-tuple-element.594, f32[2,2048]{1,0:T(2,128)S(1)} %get-tuple-element.821, pred[2048,256]{0,1:T(8,128)(4,1)S(1)} %compare_and_fusion.1, f32[2,2048]{1,0:T(2,128)S(1)} %get-tuple-element.820, ...), kind=kOutput, calls=%fused_computation.32 | convolution fusion | flops 273678336 | bytes 9076736 | tf_op jit(solution)/shard_map/while/body/eval_jaxpr/cond/branch_1_fun/hqk,hkd->hqd/dot_general | solution.py:41
  130.7 1.3 and_reduce_fusion.5
  132.7 1.0 dynamic-slice_bitcast_fusion.7
  133.8 8.8 %conditional.9 = ((f32[2,2048]{1,0:T(2,128)S(1)}, f32[2,2048]{1,0:T(2,128)S(1)}, f32[2,2048,128]{2,1,0:T(8,128)S(1)})) conditional(s32[]{:T(128)} %convert_element_type.65, (f32[2,2048]{1,0:T(2,128)S(1)}, f32[2,2048]{1,0:T(2,128)S(1)}, f32[2,2048,128]{2,1,0:T(8,128)S(1)}) %tuple.145, (s32[256]{0:T(256)S(1)}, s32[128]{0:T(128)S(1)}, ...), branch_computations={%region_14.14_spmd, %region_15.17_spmd} | conditional | flops 551051264 | bytes 38357052 | solution.py:50
  134.7 2.2 %fusion.25 = (f32[2,2048]{1,0:T(2,128)S(1)}, f32[2,2048,256]{1,2,0:T(8,128)S(1)}) fusion(pred[2048,256]{0,1:T(8,128)(4,1)S(1)} %compare_and_fusion.1, bf16[2,2048,128]{2,1,0:T(8,128)(2,1)} %get-tuple-element.591, bf16[256,2,128]{2,0,1:T(8,128)(2,1)S(1)} %copy.41), kind=kOutput, calls=%fused_computation.29 | convolution fusion | flops 271577088 | bytes 5914624 | tf_op jit(solution)/shard_map/while/body/eval_jaxpr/cond/branch_1_fun/hqd,hkd->hqk/dot_general | solution.py:31
  139.1 3.5 %convolution_add_fusion.1 = f32[2,2048,128]{2,1,0:T(8,128)S(1)} fusion(f32[2,2048,256]{1,2,0:T(8,128)} %copy-done, f32[2,2048,128]{2,1,0:T(8,128)S(1)} %get-tuple-element.594, f32[2,2048]{1,0:T(2,128)S(1)} %get-tuple-element.821, pred[2048,256]{0,1:T(8,128)(4,1)S(1)} %compare_and_fusion.1, f32[2,2048]{1,0:T(2,128)S(1)} %get-tuple-element.820, ...), kind=kOutput, calls=%fused_computation.32 | convolution fusion | flops 273678336 | bytes 9076736 | tf_op jit(solution)/shard_map/while/body/eval_jaxpr/cond/branch_1_fun/hqk,hkd->hqd/dot_general | solution.py:41
  143.4 1.7 copy.52
  145.3 1.2 copy.49
  146.6 18.2 %while.60 = (s32[]{:T(128)}, f32[2,2048]{1,0:T(2,128)S(1)}, f32[2,2048]{1,0:T(2,128)S(1)}, f32[2,2048,128]{2,1,0:T(8,128)S(1)}, s32[]{:T(128)}, /*index=5*/s32[]...) while((s32[]{:T(128)}, f32[2,2048]{1,0:T(2,128)S(1)}, ...), condition=%wide.region_10.11_spmd.clone.clone, body=%wide.region_4.10_spmd.clone.clone.sunk | while | flops 551577664 | bytes 39410428 | solution.py:113
  146.7 1.3 and_reduce_fusion.4
  148.7 1.0 dynamic-slice_bitcast_fusion.6
  149.7 8.8 %conditional.8 = ((f32[2,2048]{1,0:T(2,128)S(1)}, f32[2,2048]{1,0:T(2,128)S(1)}, f32[2,2048,128]{2,1,0:T(8,128)S(1)})) conditional(s32[]{:T(128)} %convert_element_type.64, (f32[2,2048]{1,0:T(2,128)S(1)}, f32[2,2048]{1,0:T(2,128)S(1)}, f32[2,2048,128]{2,1,0:T(8,128)S(1)}) %tuple.140, (s32[256]{0:T(256)S(1)}, s32[128]{0:T(128)S(1)}, s32[128]{0:T(128)S(1)}, ...), branch_computations={%region_6.6_spmd, %region_7.9_spmd} | conditional | flops 551051264 | bytes 38357052 | solution.py:50
  150.7 2.2 %fusion.12 = (f32[2,2048]{1,0:T(2,128)S(1)}, f32[2,2048,256]{1,2,0:T(8,128)S(1)}) fusion(pred[2048,256]{0,1:T(8,128)(4,1)S(1)} %compare_and_fusion, bf16[2,2048,128]{2,1,0:T(8,128)(2,1)} %get-tuple-element.566, bf16[256,2,128]{2,0,1:T(8,128)(2,1)S(1)} %copy.38), kind=kOutput, calls=%fused_computation.10 | convolution fusion | flops 271577088 | bytes 5914624 | tf_op jit(solution)/shard_map/while/body/eval_jaxpr/cond/branch_1_fun/hqd,hkd->hqk/dot_general | solution.py:31
  153.0 1.0 fusion.14
  155.0 3.5 %convolution_add_fusion = f32[2,2048,128]{2,1,0:T(8,128)S(1)} fusion(f32[2,2048,256]{1,2,0:T(8,128)} %copy-done.1, f32[2,2048,128]{2,1,0:T(8,128)S(1)} %get-tuple-element.569, f32[2,2048]{1,0:T(2,128)S(1)} %get-tuple-element.817, pred[2048,256]{0,1:T(8,128)(4,1)S(1)} %compare_and_fusion, f32[2,2048]{1,0:T(2,128)S(1)} %get-tuple-element.816, ...), kind=kOutput, calls=%fused_computation.13 | convolution fusion | flops 273678336 | bytes 9076736 | tf_op jit(solution)/shard_map/while/body/eval_jaxpr/cond/branch_1_fun/hqk,hkd->hqd/dot_general | solution.py:41
  158.6 1.3 and_reduce_fusion.4
  160.7 1.0 dynamic-slice_bitcast_fusion.6
  161.8 1.3 and_reduce_fusion.4
  163.8 1.0 dynamic-slice_bitcast_fusion.6
  165.6 1.7 copy.50
  167.3 1.8 pad_maximum_fusion.3
  169.1 2.9 %copy.53 = bf16[256,4096]{1,0:T(8,128)(2,1)} copy(bf16[256,4096]{0,1:T(8,128)(2,1)S(1)} %pad_maximum_fusion.3) | data formatting | bytes 4194304 | tf_op jit(solution)/shard_map/concatenate | solution.py:155
  171.9 29.3 %all_to_all.73 = bf16[4,64,4096]{2,1,0:T(8,128)(2,1)S(1)} all-to-all(bf16[4,64,4096]{2,1,0:T(8,128)(2,1)} %bitcast.103), channel_id=1, replica_groups=mesh['seq'=8,'kvh'=4] {'kvh'}, dimensions={0} | all-to-all | bytes 4194304 | tf_op jit(solution)/shard_map/all_to_all | solution.py:156
  201.2 1.5 copy.60
  (117 shorter events, 19.6 us)
Async XLA Ops:
  1.6 10.2 %all-to-all-start.1 = ((bf16[64,4,256]{2,0,1:T(8,128)(2,1)}), bf16[64,4,256]{2,0,1:T(8,128)(2,1)S(1)}, u32[]{:S(2)}, u32[]{:S(2)}) async-start(bf16[64,4,256]{2,0,1:T(8,128)(2,1)} %bitcast.85), calls=%async_computation.1 | async-start | bytes 262144 | tf_op jit(solution)/shard_map/all_to_all | solution.py:59
  7.9 7.1 %copy-start.3 = (s32[8]{0:T(128)S(1)}, s32[8]{0:T(128)}, u32[]{:S(2)}) copy-start(s32[8]{0:T(128)} %param.21) | copy-start | bytes 100
  11.7 7.9 %all-to-all-start = ((bf16[64,4,256]{2,0,1:T(8,128)(2,1)}), bf16[64,4,256]{2,0,1:T(8,128)(2,1)S(1)}, u32[]{:S(2)}, u32[]{:S(2)}) async-start(bf16[64,4,256]{2,0,1:T(8,128)(2,1)} %bitcast.86), calls=%async_computation | async-start | bytes 262144 | tf_op jit(solution)/shard_map/all_to_all | solution.py:58
  19.7 82.9 %all-to-all-start.2 = ((bf16[64,4,4096]{2,0,1:T(8,128)(2,1)}), bf16[64,4,4096]{2,0,1:T(8,128)(2,1)}, u32[]{:S(2)}, u32[]{:S(2)}) async-start(bf16[64,4,4096]{2,0,1:T(8,128)(2,1)} %bitcast.84), calls=%async_computation.2 | async-start | bytes 4194304 | tf_op jit(solution)/shard_map/all_to_all | solution.py:57
  25.1 15.2 %collective-permute-start = (bf16[256,512]{1,0:T(8,128)(2,1)S(1)}, bf16[256,512]{1,0:T(8,128)(2,1)S(1)}, u32[]{:S(2)}, u32[]{:S(2)}) collective-permute-start(bf16[256,512]{1,0:T(8,128)(2,1)S(1)} %get-tuple-element.1065), channel_id=1, source_target_pairs={{0,4},{4,8},{8,12},{12,16},{16,20},{20,24},{24,28},{1,5},{5,9},{9,... | collective-permute-start | bytes 786440 | tf_op jit(solution)/shard_map/while/body/eval_jaxpr/ppermute | solution.py:14
  28.5 13.7 %collective-permute-start.1 = (bf16[256,512]{1,0:T(8,128)(2,1)}, bf16[256,512]{1,0:T(8,128)(2,1)S(1)}, u32[]{:S(2)}, u32[]{:S(2)}) collective-permute-start(bf16[256,512]{1,0:T(8,128)(2,1)} %get-tuple-element.1066), channel_id=1, source_target_pairs={{4,0},{8,4},{12,8},{16,12},{20,16},{24,20},{28,24},{5,1},{9,5},{13... | collective-permute-start | bytes 786440 | tf_op jit(solution)/shard_map/while/body/eval_jaxpr/ppermute | solution.py:14
  42.9 11.3 %collective-permute-start = (bf16[256,512]{1,0:T(8,128)(2,1)S(1)}, bf16[256,512]{1,0:T(8,128)(2,1)S(1)}, u32[]{:S(2)}, u32[]{:S(2)}) collective-permute-start(bf16[256,512]{1,0:T(8,128)(2,1)S(1)} %get-tuple-element.1065), channel_id=1, source_target_pairs={{0,4},{4,8},{8,12},{12,16},{16,20},{20,24},{24,28},{1,5},{5,9},{9,... | collective-permute-start | bytes 786440 | tf_op jit(solution)/shard_map/while/body/eval_jaxpr/ppermute | solution.py:14
  45.5 14.2 %collective-permute-start.1 = (bf16[256,512]{1,0:T(8,128)(2,1)}, bf16[256,512]{1,0:T(8,128)(2,1)S(1)}, u32[]{:S(2)}, u32[]{:S(2)}) collective-permute-start(bf16[256,512]{1,0:T(8,128)(2,1)} %get-tuple-element.1066), channel_id=1, source_target_pairs={{4,0},{8,4},{12,8},{16,12},{20,16},{24,20},{28,24},{5,1},{9,5},{13... | collective-permute-start | bytes 786440 | tf_op jit(solution)/shard_map/while/body/eval_jaxpr/ppermute | solution.py:14
  60.5 11.1 %collective-permute-start = (bf16[256,512]{1,0:T(8,128)(2,1)S(1)}, bf16[256,512]{1,0:T(8,128)(2,1)S(1)}, u32[]{:S(2)}, u32[]{:S(2)}) collective-permute-start(bf16[256,512]{1,0:T(8,128)(2,1)S(1)} %get-tuple-element.1065), channel_id=1, source_target_pairs={{0,4},{4,8},{8,12},{12,16},{16,20},{20,24},{24,28},{1,5},{5,9},{9,... | collective-permute-start | bytes 786440 | tf_op jit(solution)/shard_map/while/body/eval_jaxpr/ppermute | solution.py:14
  62.4 14.7 %collective-permute-start.1 = (bf16[256,512]{1,0:T(8,128)(2,1)}, bf16[256,512]{1,0:T(8,128)(2,1)S(1)}, u32[]{:S(2)}, u32[]{:S(2)}) collective-permute-start(bf16[256,512]{1,0:T(8,128)(2,1)} %get-tuple-element.1066), channel_id=1, source_target_pairs={{4,0},{8,4},{12,8},{16,12},{20,16},{24,20},{28,24},{5,1},{9,5},{13... | collective-permute-start | bytes 786440 | tf_op jit(solution)/shard_map/while/body/eval_jaxpr/ppermute | solution.py:14
  77.9 11.1 %collective-permute-start = (bf16[256,512]{1,0:T(8,128)(2,1)S(1)}, bf16[256,512]{1,0:T(8,128)(2,1)S(1)}, u32[]{:S(2)}, u32[]{:S(2)}) collective-permute-start(bf16[256,512]{1,0:T(8,128)(2,1)S(1)} %get-tuple-element.1065), channel_id=1, source_target_pairs={{0,4},{4,8},{8,12},{12,16},{16,20},{20,24},{24,28},{1,5},{5,9},{9,... | collective-permute-start | bytes 786440 | tf_op jit(solution)/shard_map/while/body/eval_jaxpr/ppermute | solution.py:14
  79.8 14.7 %collective-permute-start.1 = (bf16[256,512]{1,0:T(8,128)(2,1)}, bf16[256,512]{1,0:T(8,128)(2,1)S(1)}, u32[]{:S(2)}, u32[]{:S(2)}) collective-permute-start(bf16[256,512]{1,0:T(8,128)(2,1)} %get-tuple-element.1066), channel_id=1, source_target_pairs={{4,0},{8,4},{12,8},{16,12},{20,16},{24,20},{28,24},{5,1},{9,5},{13... | collective-permute-start | bytes 786440 | tf_op jit(solution)/shard_map/while/body/eval_jaxpr/ppermute | solution.py:14
  113.1 1.9 copy-start
  125.0 1.9 copy-start
  136.9 1.9 copy-start
  143.3 1.7 copy-start.2
  152.9 1.9 copy-start.1
where the time goes:
time: 204 us; the launch traced here: 203 us
  waiting for transfers between devices  44.5 us (22%)
  local copies, waits for them, and re-layouts  41.5 us (20%)
  starting transfers between devices  38.1 us (19%)
  blocking collectives  29.3 us (14%)
  matrix products  22.9 us (11%)
  other arithmetic  21.3 us (10%)
  loops' own time  5.02 us (2%)
    ppermute x8, waiting for transfers between devices, shifted(): return lax.ppermute(block, axis, route)  40 us
    all_to_all x1, blocking collectives, on_device(): lax.all_to_all(merged, 'kvh', split_axis=0, concat_axis=1, tiled=True)  29.3 us
    ppermute x8, starting transfers between devices, shifted(): return lax.ppermute(block, axis, route)  27 us
    dot_general x4, matrix products, compute(): jnp.einsum('hqk,hkd->hqd', weights.astype(jnp.bfloat16), value_part, pref...  14.1 us
    dot_general x4, matrix products, compute(): jnp.einsum('hqd,hkd->hqk', query_block, key_part, preferred_element_type=...  8.77 us
    reduce_or x6, other arithmetic, absorb(): touched = jnp.any((key_pos >= lowest) & (key_pos <= highest))  7.91 us
    squeeze x6, local copies, waits for them, and re-layouts, fetch_whole(): lax.dynamic_slice(window, (slot, half_no * half_rows, 0), (1, half_rows,...  6 us
    all_to_all x1, waiting for transfers between devices, on_device(): lax.all_to_all(key_rows, 'kvh', split_axis=1, concat_axis=0, tiled=True)  4.5 us
  transfers between devices with their start and end apart: 11, of which 9 were waited for; matrix products, arithmetic and copies ran while one was open for 9% of the time, Pallas kernels for 0%

commit v1 on v0

v1 whole, which is shorter than its diff:
```python
import functools
import math

import jax
import jax.numpy as jnp
from jax import lax
from jax.experimental import pallas as pl
from jax.experimental.pallas import tpu as pltpu
from jax.sharding import PartitionSpec as P

DH = 128


def doc_start(position, doc_ends, doc_lengths):
    return jnp.sum(
        jnp.where(doc_ends[None, :] <= position[:, None], doc_lengths[None, :], 0), axis=1
    )


def attend_kernel(
    blocks_ref, q_ref, start_ref, kv_hbm, out_ref, k_buf, v_buf, sems,
    *, half_rows, group_size, kv_feat, pad_rows, window
):
    side = pl.program_id(0)
    head = pl.program_id(1)
    block_id = blocks_ref[side]
    first = pl.multiple_of(block_id * half_rows, half_rows)
    k_copy = pltpu.make_async_copy(
        kv_hbm.at[pl.ds(first, window), pl.ds(pl.multiple_of(head * DH, DH), DH)],
        k_buf,
        sems.at[0],
    )
    v_copy = pltpu.make_async_copy(
        kv_hbm.at[pl.ds(first, window), pl.ds(pl.multiple_of(kv_feat + head * DH, DH), DH)],
        v_buf,
        sems.at[1],
    )
    k_copy.start()
    v_copy.start()
    row_pos = block_id * half_rows + lax.broadcasted_iota(jnp.int32, (half_rows, window), 0)
    key_pos = block_id * half_rows - pad_rows + lax.broadcasted_iota(
        jnp.int32, (half_rows, window), 1
    )
    row_start = start_ref[...]
    allowed = (key_pos <= row_pos) & (key_pos >= row_start)
    bias = jnp.where(allowed, 0.0, -jnp.inf).astype(jnp.float32)
    k_copy.wait()
    v_copy.wait()
    scale = 1.0 / math.sqrt(DH)

    def one_member(g, carry):
        col = pl.multiple_of(g * DH, DH)
        q_g = q_ref[:, pl.ds(col, DH)]
        scores = lax.dot_general(
            q_g, k_buf[...], (((1,), (1,)), ((), ())), preferred_element_type=jnp.float32
        )
        scores = scores * scale + bias
        top = jnp.max(scores, axis=1, keepdims=True)
        weights = jnp.exp(scores - top)
        total = jnp.sum(weights, axis=1, keepdims=True)
        mixed = jnp.dot(
            weights.astype(jnp.bfloat16), v_buf[...], preferred_element_type=jnp.float32
        )
        out_ref[:, pl.ds(col, DH)] = (mixed / total).astype(out_ref.dtype)
        return carry

    lax.fori_loop(0, group_size, one_member, 0)


def on_device(queries, key_rows, value_rows, doc_lengths):
    shards = lax.axis_size("seq")
    kvh = lax.axis_size("kvh")
    my_shard = lax.axis_index("seq")
    rows_in = key_rows.shape[0]
    head_queries = lax.all_to_all(queries, "kvh", split_axis=1, concat_axis=0, tiled=True)
    kv_cols = key_rows.shape[1] // kvh
    kv_local = jnp.concatenate(
        [key_rows.reshape(rows_in, kvh, kv_cols), value_rows.reshape(rows_in, kvh, kv_cols)],
        axis=2,
    )
    kv_slab = lax.all_to_all(kv_local, "kvh", split_axis=1, concat_axis=0, tiled=True)
    dev_rows = kv_slab.shape[0]
    kv_slab = kv_slab.reshape(dev_rows, 2 * kv_cols)
    half_rows = dev_rows // 2
    kv_feat = kv_cols
    kv_heads = kv_feat // DH
    group_size = head_queries.shape[1] // kv_feat
    seq_total = dev_rows * shards
    longest = min(13 * half_rows, seq_total // 4)
    lookback = (longest + half_rows - 2) // half_rows
    pad_rows = lookback * half_rows
    window = pad_rows + half_rows

    gathered = lax.all_gather(kv_slab, "seq", axis=0, tiled=False)
    low = gathered[:, :half_rows].reshape(shards * half_rows, 2 * kv_feat)
    high = gathered[::-1, half_rows:].reshape(shards * half_rows, 2 * kv_feat)
    kv_pos = jnp.concatenate(
        [jnp.zeros((pad_rows, 2 * kv_feat), kv_slab.dtype), low, high], axis=0
    )

    doc_ends = jnp.cumsum(doc_lengths)
    block_ids = jnp.stack([my_shard, 2 * shards - 1 - my_shard]).astype(jnp.int32)
    positions = block_ids[:, None] * half_rows + jnp.arange(half_rows, dtype=jnp.int32)[None, :]
    starts = doc_start(positions.reshape(-1), doc_ends, doc_lengths).astype(jnp.int32)
    starts = starts.reshape(2, half_rows, 1)

    kernel = functools.partial(
        attend_kernel,
        half_rows=half_rows,
        group_size=group_size,
        kv_feat=kv_feat,
        pad_rows=pad_rows,
        window=window,
    )
    q_cols = group_size * DH
    merged = pl.pallas_call(
        kernel,
        out_shape=jax.ShapeDtypeStruct(head_queries.shape, head_queries.dtype),
        grid_spec=pltpu.PrefetchScalarGridSpec(
            num_scalar_prefetch=1,
            grid=(2, kv_heads),
            in_specs=[
                pl.BlockSpec((half_rows, q_cols), lambda s, h, b: (s, h)),
                pl.BlockSpec((None, half_rows, 1), lambda s, h, b: (s, 0, 0)),
                pl.BlockSpec(memory_space=pl.ANY),
            ],
            out_specs=pl.BlockSpec((half_rows, q_cols), lambda s, h, b: (s, h)),
            scratch_shapes=[
                pltpu.VMEM((window, DH), kv_slab.dtype),
                pltpu.VMEM((window, DH), kv_slab.dtype),
                pltpu.SemaphoreType.DMA((2,)),
            ],
        ),
    )(block_ids, head_queries, starts, kv_pos)
    return lax.all_to_all(merged, "kvh", split_axis=0, concat_axis=1, tiled=True)


def solution(mesh):
    return jax.shard_map(
        on_device,
        mesh=mesh,
        in_specs=(P(("seq", "kvh"), None), P(("seq", "kvh"), None), P(("seq", "kvh"), None), P()),
        out_specs=P(("seq", "kvh"), None),
        check_vma=False,
    )
```

time: 204 us -> 154 us (0.75)
  the two profiles are of different devices: /device:TPU:8 before, /device:TPU:0 now
where the time goes in v1:
time: 154 us
  waiting for transfers between devices  43.1 us (28%)
  blocking collectives  39.5 us (26%)
  Pallas kernels  38 us (25%)
  between operations  13.5 us (9%)
  local copies, waits for them, and re-layouts  11.6 us (8%)
  other arithmetic  4.38 us (3%)
  starting transfers between devices  3.74 us (2%)
    all_gather x1, waiting for transfers between devices, on_device(): gathered = lax.all_gather(kv_slab, 'seq', axis=0, tiled=False)  43.1 us
    pallas_call x1, Pallas kernels, on_device(): pl.pallas_call(kernel, out_shape=jax.ShapeDtypeStruct(head_queries.shape,...  38 us
    all_to_all x1, blocking collectives, on_device(): lax.all_to_all(merged, 'kvh', split_axis=0, concat_axis=1, tiled=True)  29.3 us
    all_to_all x1, blocking collectives, on_device(): lax.all_to_all(kv_local, 'kvh', split_axis=1, concat_axis=0, tiled=True)  10.2 us
    all_to_all x1, starting transfers between devices, on_device(): lax.all_to_all(queries, 'kvh', split_axis=1, concat_axis=0, tiled=True)  3.74 us
    concatenate x1, other arithmetic, on_device(): jnp.concatenate([jnp.zeros((pad_rows, 2 * kv_feat), kv_slab.dtype), low,...  3.26 us
  transfers between devices with their start and end apart: 2, of which 1 were waited for; matrix products, arithmetic and copies ran while one was open for 7% of the time, Pallas kernels for 0%

profile of v1, /device:TPU:0, one launch (start us, length us, event | category | flops | bytes accessed | tf_op | source)
XLA Modules:
  0.0 153.7 jit_solution(5530878572072378849)
XLA Ops:
  6.5 0.0 copy-start.1
  6.5 0.0 all-gather.2.cloned.1.call-start
  6.5 1.1 reshape.83
  7.7 1.0 reshape.82
  8.7 0.1 pad_maximum_fusion.1
  8.8 10.2 %all_to_all.53 = bf16[64,4,512]{2,0,1:T(8,128)(2,1)} all-to-all(bf16[64,4,512]{2,0,1:T(8,128)(2,1)S(1)} %copy.20), channel_id=1, replica_groups=mesh['seq'=8,'kvh'=4] {'kvh'}, dimensions={1} | all-to-all | bytes 524288 | tf_op jit(solution)/shard_map/all_to_all | solution.py:81
  19.0 0.0 all-gather.2.cloned.1.call-update
  19.0 0.0 copy-done.1
  19.1 1.5 copy.26
  20.5 0.0 copy-start.2
  20.5 3.7 %all-to-all-start = ((bf16[64,4,4096]{2,0,1:T(8,128)(2,1)}), bf16[64,4,4096]{2,0,1:T(8,128)(2,1)S(1)}, u32[]{:S(2)}, u32[]{:S(2)}) async-start(bf16[64,4,4096]{2,0,1:T(8,128)(2,1)} %bitcast.26), calls=%async_computation | async-start | bytes 4194304 | tf_op jit(solution)/shard_map/all_to_all | solution.py:75
  24.3 0.0 copy-done.2
  24.3 0.2 reduce-window.8
  24.5 0.7 broadcast_multiply_fusion
  25.1 0.1 add_bitcast_fusion
  25.2 0.1 select_reduce_fusion
  25.3 0.8 copy.21.start_ref
  26.1 43.1 %all-gather.2.cloned.1.call-done = bf16[8,256,512]{2,1,0:T(8,128)(2,1)} async-done(((bf16[1,256,512]{2,1,0:T(8,128)(2,1)}), bf16[8,256,512]{2,1,0:T(8,128)(2,1)}) %all-gather.2.cloned.1.call-update) | async-done | bytes 2097168 | tf_op jit(solution)/shard_map/all_gather | solution.py:94
  69.1 3.1 %fusion = (bf16[8,128,512]{2,1,0:T(8,128)(2,1)}, bf16[8,128,512]{2,1,0:T(8,128)(2,1)}) fusion(bf16[8,256,512]{2,1,0:T(8,128)(2,1)} %all-gather.2.cloned.1.call-done), kind=kLoop, calls=%fused_computation.7 | loop fusion | bytes 4194304 | tf_op jit(solution)/shard_map/slice | solution.py:95
  72.2 1.3 rev.3
  73.5 3.3 %pad_maximum_fusion.kv_hbm = bf16[2560,512]{1,0:T(8,128)(2,1)} fusion(bf16[1024,512]{1,0:T(8,128)(2,1)S(1)} %bitcast.29, bf16[1024,512]{1,0:T(8,128)(2,1)} %bitcast.30, bf16[2560]{0:T(1024)(128)(2,1)S(1)} %pad.clone), kind=kLoop, calls=%fused_computation | loop fusion | flops 7864320 | bytes 4723712 | tf_op jit(solution)/shard_map/concatenate | solution.py:97
  76.8 0.0 all-to-all-done
  76.8 0.0 copy-start
  76.8 1.3 copy-done
  78.1 38.0 %shard_map.46 = bf16[256,4096]{1,0:T(8,128)(2,1)} custom-call(s32[2]{0:T(128)} %get-tuple-element.6.blocks_ref, bf16[256,4096]{1,0:T(8,128)(2,1)} %bitcast.25, s32[2,128,1]{2,1,0:T(8,128)} %copy.21.start_ref, bf16[2560,512]{1,0:T(8,128)(2,1)} %pad_maximum_fusion.kv_hbm), custom_call_target="tpu_custom_call" | custom-call | tf_op jit(solution)/shard_map/pallas_call | solution.py:116
  116.1 29.3 %all_to_all.54 = bf16[4,64,4096]{2,1,0:T(8,128)(2,1)S(1)} all-to-all(bf16[4,64,4096]{2,1,0:T(8,128)(2,1)} %bitcast.27), channel_id=1, replica_groups=mesh['seq'=8,'kvh'=4] {'kvh'}, dimensions={0} | all-to-all | bytes 4194304 | tf_op jit(solution)/shard_map/all_to_all | solution.py:135
  145.4 1.5 copy.24
  (3 shorter events, 0.1 us)
Async XLA Ops:
  6.5 12.5 %copy-start.1 = (bf16[64,16384]{1,0:T(8,128)(2,1)S(1)}, bf16[64,16384]{1,0:T(8,128)(2,1)}, u32[]{:S(2)}) copy-start(bf16[64,16384]{1,0:T(8,128)(2,1)} %param.4) | copy-start | bytes 6291460
  6.5 62.6 %all-gather.2.cloned.1.call-start = ((), (), s32[]{:S(2)}) async-start(), calls=%async_computation.3 | async-start | bytes 2359296 | tf_op jit(solution)/shard_map/all_gather | solution.py:94
  20.5 3.8 %copy-start.2 = (s32[8]{0:T(128)S(1)}, s32[8]{0:T(128)}, u32[]{:S(2)}) copy-start(s32[8]{0:T(128)} %param.7) | copy-start | bytes 100
  20.5 56.3 %all-to-all-start = ((bf16[64,4,4096]{2,0,1:T(8,128)(2,1)}), bf16[64,4,4096]{2,0,1:T(8,128)(2,1)S(1)}, u32[]{:S(2)}, u32[]{:S(2)}) async-start(bf16[64,4,4096]{2,0,1:T(8,128)(2,1)} %bitcast.26), calls=%async_computation | async-start | bytes 4194304 | tf_op jit(solution)/shard_map/all_to_all | solution.py:75
  76.8 1.3 copy-start
Sparse Core Ops, SparseCore 0:
  19.2 49.9 all-gather.1

commit v2 on v1

--- a/solution.py
+++ b/solution.py
@@ -11,6 +11,12 @@
 DH = 128
 
 
+def shifted(block, axis, distance):
+    devices = range(lax.axis_size(axis))
+    route = [(i - distance, i) for i in devices if i - distance in devices]
+    return lax.ppermute(block, axis, route)
+
+
 def doc_start(position, doc_ends, doc_lengths):
     return jnp.sum(
         jnp.where(doc_ends[None, :] <= position[:, None], doc_lengths[None, :], 0), axis=1
@@ -18,25 +24,11 @@
 
 
 def attend_kernel(
-    blocks_ref, q_ref, start_ref, kv_hbm, out_ref, k_buf, v_buf, sems,
-    *, half_rows, group_size, kv_feat, pad_rows, window
+    blocks_ref, q_ref, start_ref, k_ref, v_ref, out_ref, kt_buf,
+    *, half_rows, group_size, pad_rows, window
 ):
     side = pl.program_id(0)
-    head = pl.program_id(1)
     block_id = blocks_ref[side]
-    first = pl.multiple_of(block_id * half_rows, half_rows)
-    k_copy = pltpu.make_async_copy(
-        kv_hbm.at[pl.ds(first, window), pl.ds(pl.multiple_of(head * DH, DH), DH)],
-        k_buf,
-        sems.at[0],
-    )
-    v_copy = pltpu.make_async_copy(
-        kv_hbm.at[pl.ds(first, window), pl.ds(pl.multiple_of(kv_feat + head * DH, DH), DH)],
-        v_buf,
-        sems.at[1],
-    )
-    k_copy.start()
-    v_copy.start()
     row_pos = block_id * half_rows + lax.broadcasted_iota(jnp.int32, (half_rows, window), 0)
     key_pos = block_id * half_rows - pad_rows + lax.broadcasted_iota(
         jnp.int32, (half_rows, window), 1
@@ -44,22 +36,19 @@
     row_start = start_ref[...]
     allowed = (key_pos <= row_pos) & (key_pos >= row_start)
     bias = jnp.where(allowed, 0.0, -jnp.inf).astype(jnp.float32)
-    k_copy.wait()
-    v_copy.wait()
+    kt_buf[...] = k_ref[...].T
     scale = 1.0 / math.sqrt(DH)
 
     def one_member(g, carry):
         col = pl.multiple_of(g * DH, DH)
         q_g = q_ref[:, pl.ds(col, DH)]
-        scores = lax.dot_general(
-            q_g, k_buf[...], (((1,), (1,)), ((), ())), preferred_element_type=jnp.float32
-        )
+        scores = jnp.dot(q_g, kt_buf[...], preferred_element_type=jnp.float32)
         scores = scores * scale + bias
         top = jnp.max(scores, axis=1, keepdims=True)
         weights = jnp.exp(scores - top)
         total = jnp.sum(weights, axis=1, keepdims=True)
         mixed = jnp.dot(
-            weights.astype(jnp.bfloat16), v_buf[...], preferred_element_type=jnp.float32
+            weights.astype(jnp.bfloat16), v_ref[...], preferred_element_type=jnp.float32
         )
         out_ref[:, pl.ds(col, DH)] = (mixed / total).astype(out_ref.dtype)
         return carry
@@ -91,11 +80,25 @@
     pad_rows = lookback * half_rows
     window = pad_rows + half_rows
 
-    gathered = lax.all_gather(kv_slab, "seq", axis=0, tiled=False)
-    low = gathered[:, :half_rows].reshape(shards * half_rows, 2 * kv_feat)
-    high = gathered[::-1, half_rows:].reshape(shards * half_rows, 2 * kv_feat)
-    kv_pos = jnp.concatenate(
-        [jnp.zeros((pad_rows, 2 * kv_feat), kv_slab.dtype), low, high], axis=0
+    first_half = kv_slab[:half_rows]
+    second_half = kv_slab[half_rows:]
+    blank = jnp.zeros_like(first_half)
+    low_side = [first_half]
+    high_side = [second_half]
+    for back in range(1, lookback + 1):
+        from_low = shifted(first_half, "seq", back)
+        from_high = shifted(second_half, "seq", -back)
+        mirror = [(t, 2 * shards - 1 - back - t) for t in range(shards)]
+        mirror = [(t, u) for t, u in mirror if 0 <= u < shards and u != t]
+        from_mirror = lax.ppermute(first_half, "seq", mirror) if mirror else blank
+        wanted = 2 * shards - 1 - my_shard - back
+        high_pick = jnp.where(
+            wanted >= shards, from_high, jnp.where(wanted == my_shard, first_half, from_mirror)
+        )
+        low_side.append(from_low)
+        high_side.append(high_pick)
+    windows = jnp.stack(
+        [jnp.concatenate(low_side[::-1], axis=0), jnp.concatenate(high_side[::-1], axis=0)]
     )
 
     doc_ends = jnp.cumsum(doc_lengths)
@@ -108,7 +111,6 @@
         attend_kernel,
         half_rows=half_rows,
         group_size=group_size,
-        kv_feat=kv_feat,
         pad_rows=pad_rows,
         window=window,
     )
@@ -122,16 +124,15 @@
             in_specs=[
                 pl.BlockSpec((half_rows, q_cols), lambda s, h, b: (s, h)),
                 pl.BlockSpec((None, half_rows, 1), lambda s, h, b: (s, 0, 0)),
-                pl.BlockSpec(memory_space=pl.ANY),
+                pl.BlockSpec((None, window, DH), lambda s, h, b: (s, 0, h)),
+                pl.BlockSpec((None, window, DH), lambda s, h, b, n=kv_heads: (s, 0, n + h)),
             ],
             out_specs=pl.BlockSpec((half_rows, q_cols), lambda s, h, b: (s, h)),
             scratch_shapes=[
-                pltpu.VMEM((window, DH), kv_slab.dtype),
-                pltpu.VMEM((window, DH), kv_slab.dtype),
-                pltpu.SemaphoreType.DMA((2,)),
+                pltpu.VMEM((DH, window), kv_slab.dtype),
             ],
         ),
-    )(block_ids, head_queries, starts, kv_pos)
+    )(block_ids, head_queries, starts, windows, windows)
     return lax.all_to_all(merged, "kvh", split_axis=0, concat_axis=1, tiled=True)
 
 

time: 154 us -> 128 us (0.83)
  starting transfers between devices: 3.74 us -> 35.6 us
  waiting for transfers between devices: 43.1 us -> 18.2 us
  between operations: 13.5 us -> 0.23 us
  blocking collectives: 39.5 us -> 29.3 us
  Pallas kernels: 38 us -> 33 us
  local copies, waits for them, and re-layouts: 11.6 us -> 7.83 us
    all_gather x1 -> x0, waiting for transfers between devices: 43.1 us -> none  [on_device(): gathered = lax.all_gather(kv_slab, 'seq', axis=0, tiled=False)]
    ppermute x0 -> x11, starting transfers between devices: none -> 27.6 us  [the longest x8 25.6 us: shifted(): return lax.ppermute(block, axis, route)]
    ppermute x0 -> x11, waiting for transfers between devices: none -> 15.9 us  [the longest x8 15.9 us: shifted(): return lax.ppermute(block, axis, route)]
    all_to_all x1 -> x0, blocking collectives: 10.2 us -> none  [on_device(): lax.all_to_all(kv_local, 'kvh', split_axis=1, concat_axis=0, tiled=True)]
    pallas_call x1, Pallas kernels: 38 us -> 33 us  [on_device(): pl.pallas_call(kernel, out_shape=jax.ShapeDtypeStruct(head_queries.shape,...]
    all_to_all x0 -> x1, starting transfers between devices: none -> 4.24 us  [on_device(): lax.all_to_all(kv_local, 'kvh', split_axis=1, concat_axis=0, tiled=True)]
    concatenate x1, other arithmetic: 3.26 us -> 0.04 us  [on_device(): jnp.concatenate(low_side[::-1], axis=0)]
    slice x1, local copies, waits for them, and re-layouts: 3.05 us -> 0.02 us  [on_device(): first_half = kv_slab[:half_rows]]
  transfers between devices with their start and end apart: 2 -> 13, of which waited for: 1 -> 5; matrix products, arithmetic and copies ran while one was open for 7% -> 5% of each run, Pallas kernels for 0% -> 0%
where the time goes in v2:
time: 128 us; the launch traced here: 127 us
  starting transfers between devices  35.6 us (28%)
  Pallas kernels  33 us (26%)
  blocking collectives  29.3 us (23%)
  waiting for transfers between devices  18.2 us (14%)
  local copies, waits for them, and re-layouts  7.83 us (6%)
  other arithmetic  3.11 us (2%)
    pallas_call x1, Pallas kernels, on_device(): pl.pallas_call(kernel, out_shape=jax.ShapeDtypeStruct(head_queries.shape,...  33 us
    all_to_all x1, blocking collectives, on_device(): lax.all_to_all(merged, 'kvh', split_axis=0, concat_axis=1, tiled=True)  29.3 us
    ppermute x8, starting transfers between devices, shifted(): return lax.ppermute(block, axis, route)  25.6 us
    ppermute x8, waiting for transfers between devices, shifted(): return lax.ppermute(block, axis, route)  15.9 us
    all_to_all x1, starting transfers between devices, on_device(): lax.all_to_all(kv_local, 'kvh', split_axis=1, concat_axis=0, tiled=True)  4.24 us
    all_to_all x1, starting transfers between devices, on_device(): lax.all_to_all(queries, 'kvh', split_axis=1, concat_axis=0, tiled=True)  3.74 us
    all_to_all x1, local copies, waits for them, and re-layouts, on_device(): lax.all_to_all(queries, 'kvh', split_axis=1, concat_axis=0, tiled=True)  3.13 us
  transfers between devices with their start and end apart: 13, of which 5 were waited for; matrix products, arithmetic and copies ran while one was open for 5% of the time, Pallas kernels for 0%

profile of v2, /device:TPU:0, one launch (start us, length us, event | category | flops | bytes accessed | tf_op | source)
XLA Modules:
  0.0 127.2 jit_solution(4857670620215753998)
XLA Ops:
  0.0 1.0 copy_bitcast_fusion.1
  1.0 0.7 pad_maximum_fusion.1
  1.7 4.2 %all-to-all-start.1 = ((bf16[64,4,512]{2,0,1:T(8,128)(2,1)}), bf16[64,4,512]{2,0,1:T(8,128)(2,1)S(1)}, u32[]{:S(2)}, u32[]{:S(2)}) async-start(bf16[64,4,512]{2,0,1:T(8,128)(2,1)} %pad_maximum_fusion.1), calls=%async_computation.1 | async-start | bytes 524288 | tf_op jit(solution)/shard_map/all_to_all | solution.py:70
  5.9 3.1 %copy.26 = bf16[8,4,8,4096]{3,2,0,1:T(8,128)(2,1)} copy(bf16[8,4,8,4096]{3,2,1,0:T(8,128)(2,1)} %bitcast.45) | data formatting | bytes 4194304 | tf_op jit(solution)/shard_map/all_to_all | solution.py:64
  9.1 0.6 broadcast_multiply_fusion
  9.7 2.3 %all-to-all-done.1 = bf16[64,4,512]{2,0,1:T(8,128)(2,1)S(1)} async-done(((bf16[64,4,512]{2,0,1:T(8,128)(2,1)}), bf16[64,4,512]{2,0,1:T(8,128)(2,1)S(1)}, u32[]{:S(2)}, u32[]{:S(2)}) %all-to-all-start.1) | async-done | bytes 262176 | tf_op jit(solution)/shard_map/all_to_all | solution.py:70
  12.0 0.0 copy-start.1
  12.0 3.7 %all-to-all-start = ((bf16[64,4,4096]{2,0,1:T(8,128)(2,1)}), bf16[64,4,4096]{2,0,1:T(8,128)(2,1)S(1)}, u32[]{:S(2)}, u32[]{:S(2)}) async-start(bf16[64,4,4096]{2,0,1:T(8,128)(2,1)} %bitcast.30), calls=%async_computation | async-start | bytes 4194304 | tf_op jit(solution)/shard_map/all_to_all | solution.py:64
  15.8 1.3 %collective-permute-start.4 = (bf16[128,512]{1,0:T(8,128)(2,1)S(1)}, bf16[128,512]{1,0:T(8,128)(2,1)S(1)}, u32[]{:S(2)}, u32[]{:S(2)}) collective-permute-start(bf16[128,512]{1,0:T(8,128)(2,1)S(1)} %bitcast.49), channel_id=1, source_target_pairs={{16,0},{20,4},{24,8},{28,12},{17,1},{21,5},{25,9},{29,13},{18,2},{... | collective-permute-start | bytes 393224 | tf_op jit(solution)/shard_map/ppermute | solution.py:17
  17.1 0.7 collective-permute-start.5
  17.7 0.1 add_bitcast_fusion
  17.8 0.0 copy-done.1
  17.8 0.2 reduce-window.8
  18.0 0.1 select_reduce_fusion
  18.1 0.8 copy.17.start_ref
  18.9 9.8 %collective-permute-start = (bf16[128,512]{1,0:T(8,128)(2,1)S(1)}, bf16[128,512]{1,0:T(8,128)(2,1)S(1)}, u32[]{:S(2)}, u32[]{:S(2)}) collective-permute-start(bf16[128,512]{1,0:T(8,128)(2,1)S(1)} %bitcast.35), channel_id=1, source_target_pairs={{0,16},{4,20},{8,24},{12,28},{1,17},{5,21},{9,25},{13,29},{2,18},{... | collective-permute-start | bytes 393224 | tf_op jit(solution)/shard_map/ppermute | solution.py:17
  28.6 1.9 %collective-permute-start.1 = (bf16[128,512]{1,0:T(8,128)(2,1)S(1)}, bf16[128,512]{1,0:T(8,128)(2,1)S(1)}, u32[]{:S(2)}, u32[]{:S(2)}) collective-permute-start(bf16[128,512]{1,0:T(8,128)(2,1)S(1)} %bitcast.36), channel_id=1, source_target_pairs={{0,12},{4,16},{8,20},{12,24},{16,28},{1,13},{5,17},{9,21},{13,25},... | collective-permute-start | bytes 393224 | tf_op jit(solution)/shard_map/ppermute | solution.py:17
  30.6 1.8 %collective-permute-start.2 = (bf16[128,512]{1,0:T(8,128)(2,1)S(1)}, bf16[128,512]{1,0:T(8,128)(2,1)S(1)}, u32[]{:S(2)}, u32[]{:S(2)}) collective-permute-start(bf16[128,512]{1,0:T(8,128)(2,1)S(1)} %bitcast.37), channel_id=1, source_target_pairs={{0,8},{4,12},{8,16},{12,20},{16,24},{20,28},{1,9},{5,13},{9,17},{1... | collective-permute-start | bytes 393224 | tf_op jit(solution)/shard_map/ppermute | solution.py:17
  32.4 0.0 collective-permute-done.4
  32.4 1.3 %collective-permute-start.6 = (bf16[128,512]{1,0:T(8,128)(2,1)S(1)}, bf16[128,512]{1,0:T(8,128)(2,1)S(1)}, u32[]{:S(2)}, u32[]{:S(2)}) collective-permute-start(bf16[128,512]{1,0:T(8,128)(2,1)S(1)} %bitcast.50), channel_id=1, source_target_pairs={{12,0},{16,4},{20,8},{24,12},{28,16},{13,1},{17,5},{21,9},{25,13},... | collective-permute-start | bytes 393224 | tf_op jit(solution)/shard_map/ppermute | solution.py:17
  33.7 0.0 collective-permute-done.5
  33.7 0.7 collective-permute-start.7
  34.4 0.1 select_dynamic-update-slice_fusion.3
  34.5 5.7 %collective-permute-done.6 = bf16[128,512]{1,0:T(8,128)(2,1)S(1)} collective-permute-done((bf16[128,512]{1,0:T(8,128)(2,1)S(1)}, bf16[128,512]{1,0:T(8,128)(2,1)S(1)}, u32[]{:S(2)}, u32[]{:S(2)}) %collective-permute-start.6) | collective-permute-done | bytes 131104 | tf_op jit(solution)/shard_map/ppermute | solution.py:17
  40.2 1.3 %collective-permute-start.8 = (bf16[128,512]{1,0:T(8,128)(2,1)S(1)}, bf16[128,512]{1,0:T(8,128)(2,1)S(1)}, u32[]{:S(2)}, u32[]{:S(2)}) collective-permute-start(bf16[128,512]{1,0:T(8,128)(2,1)S(1)} %bitcast.51), channel_id=1, source_target_pairs={{8,0},{12,4},{16,8},{20,12},{24,16},{28,20},{9,1},{13,5},{17,9},{2... | collective-permute-start | bytes 393224 | tf_op jit(solution)/shard_map/ppermute | solution.py:17
  41.5 0.0 collective-permute-done.7
  41.5 0.7 collective-permute-start.9
  42.2 0.1 select_dynamic-update-slice_fusion.2
  42.2 4.8 %collective-permute-done.8 = bf16[128,512]{1,0:T(8,128)(2,1)S(1)} collective-permute-done((bf16[128,512]{1,0:T(8,128)(2,1)S(1)}, bf16[128,512]{1,0:T(8,128)(2,1)S(1)}, u32[]{:S(2)}, u32[]{:S(2)}) %collective-permute-start.8) | collective-permute-done | bytes 131104 | tf_op jit(solution)/shard_map/ppermute | solution.py:17
  47.0 6.9 %collective-permute-start.3 = (bf16[128,512]{1,0:T(8,128)(2,1)S(1)}, bf16[128,512]{1,0:T(8,128)(2,1)S(1)}, u32[]{:S(2)}, u32[]{:S(2)}) collective-permute-start(bf16[128,512]{1,0:T(8,128)(2,1)S(1)} %bitcast.42), channel_id=1, source_target_pairs={{0,4},{4,8},{8,12},{12,16},{16,20},{20,24},{24,28},{1,5},{5,9},{9,... | collective-permute-start | bytes 393224 | tf_op jit(solution)/shard_map/ppermute | solution.py:17
  54.0 0.0 collective-permute-done.9
  54.0 1.3 %collective-permute-start.10 = (bf16[128,512]{1,0:T(8,128)(2,1)S(1)}, bf16[128,512]{1,0:T(8,128)(2,1)S(1)}, u32[]{:S(2)}, u32[]{:S(2)}) collective-permute-start(bf16[128,512]{1,0:T(8,128)(2,1)S(1)} %bitcast.52), channel_id=1, source_target_pairs={{4,0},{8,4},{12,8},{16,12},{20,16},{24,20},{28,24},{5,1},{9,5},{13... | collective-permute-start | bytes 393224 | tf_op jit(solution)/shard_map/ppermute | solution.py:17
  55.3 0.1 select_dynamic-update-slice_fusion.1
  55.3 0.0 collective-permute-done
  55.4 0.0 collective-permute-done.1
  55.4 0.0 collective-permute-done.2
  55.4 2.4 %collective-permute-done.3 = bf16[128,512]{1,0:T(8,128)(2,1)S(1)} collective-permute-done((bf16[128,512]{1,0:T(8,128)(2,1)S(1)}, bf16[128,512]{1,0:T(8,128)(2,1)S(1)}, u32[]{:S(2)}, u32[]{:S(2)}) %collective-permute-start.3) | collective-permute-done | bytes 131104 | tf_op jit(solution)/shard_map/ppermute | solution.py:17
  57.9 3.0 %collective-permute-done.10 = bf16[128,512]{1,0:T(8,128)(2,1)S(1)} collective-permute-done((bf16[128,512]{1,0:T(8,128)(2,1)S(1)}, bf16[128,512]{1,0:T(8,128)(2,1)S(1)}, u32[]{:S(2)}, u32[]{:S(2)}) %collective-permute-start.10) | collective-permute-done | bytes 131104 | tf_op jit(solution)/shard_map/ppermute | solution.py:17
  60.9 1.2 pad_maximum_fusion.k_ref.v_ref
  62.1 0.0 all-to-all-done
  62.1 0.0 copy-start
  62.1 1.3 %copy-done = bf16[64,4,4096]{2,0,1:T(8,128)(2,1)} copy-done((bf16[64,4,4096]{2,0,1:T(8,128)(2,1)}, bf16[64,4,4096]{2,0,1:T(8,128)(2,1)S(1)}, u32[]{:S(2)}) %copy-start) | copy-done | bytes 2097176
  63.4 33.0 %shard_map.46 = bf16[256,4096]{1,0:T(8,128)(2,1)} custom-call(s32[2]{0:T(128)} %get-tuple-element.6.blocks_ref, bf16[256,4096]{1,0:T(8,128)(2,1)} %bitcast.31, s32[2,128,1]{2,1,0:T(8,128)} %copy.17.start_ref, bf16[2,640,512]{2,1,0:T(8,128)(2,1)} %pad_maximum_fusion.k_ref.v_ref, bf16[2,640,512]{2,1,0:T(8,128)(2,1)} %pad_maximum_fusion.k_ref.v_ref), custom_call_target="tpu_custom_call" | custom-call | tf_op jit(solution)/shard_map/pallas_call | solution.py:118
  96.4 29.3 %all_to_all.53 = bf16[4,64,4096]{2,1,0:T(8,128)(2,1)S(1)} all-to-all(bf16[4,64,4096]{2,1,0:T(8,128)(2,1)} %bitcast.32), channel_id=1, replica_groups=mesh['seq'=8,'kvh'=4] {'kvh'}, dimensions={0} | all-to-all | bytes 4194304 | tf_op jit(solution)/shard_map/all_to_all | solution.py:136
  125.7 1.5 %copy.22 = bf16[4,8,8,4096]{3,2,0,1:T(8,128)(2,1)} copy(bf16[4,8,8,4096]{3,2,1,0:T(8,128)(2,1)S(1)} %bitcast.33) | data formatting | bytes 4194304 | tf_op jit(solution)/shard_map/all_to_all | solution.py:136
  (7 shorter events, 0.1 us)
Async XLA Ops:
  1.7 10.3 %all-to-all-start.1 = ((bf16[64,4,512]{2,0,1:T(8,128)(2,1)}), bf16[64,4,512]{2,0,1:T(8,128)(2,1)S(1)}, u32[]{:S(2)}, u32[]{:S(2)}) async-start(bf16[64,4,512]{2,0,1:T(8,128)(2,1)} %pad_maximum_fusion.1), calls=%async_computation.1 | async-start | bytes 524288 | tf_op jit(solution)/shard_map/all_to_all | solution.py:70
  12.0 5.8 %copy-start.1 = (s32[8]{0:T(128)S(1)}, s32[8]{0:T(128)}, u32[]{:S(2)}) copy-start(s32[8]{0:T(128)} %param.7) | copy-start | bytes 100
  12.0 50.1 %all-to-all-start = ((bf16[64,4,4096]{2,0,1:T(8,128)(2,1)}), bf16[64,4,4096]{2,0,1:T(8,128)(2,1)S(1)}, u32[]{:S(2)}, u32[]{:S(2)}) async-start(bf16[64,4,4096]{2,0,1:T(8,128)(2,1)} %bitcast.30), calls=%async_computation | async-start | bytes 4194304 | tf_op jit(solution)/shard_map/all_to_all | solution.py:64
  15.8 16.6 %collective-permute-start.4 = (bf16[128,512]{1,0:T(8,128)(2,1)S(1)}, bf16[128,512]{1,0:T(8,128)(2,1)S(1)}, u32[]{:S(2)}, u32[]{:S(2)}) collective-permute-start(bf16[128,512]{1,0:T(8,128)(2,1)S(1)} %bitcast.49), channel_id=1, source_target_pairs={{16,0},{20,4},{24,8},{28,12},{17,1},{21,5},{25,9},{29,13},{18,2},{... | collective-permute-start | bytes 393224 | tf_op jit(solution)/shard_map/ppermute | solution.py:17
  17.1 16.7 %collective-permute-start.5 = (bf16[128,512]{1,0:T(8,128)(2,1)S(1)}, bf16[128,512]{1,0:T(8,128)(2,1)S(1)}, u32[]{:S(2)}, u32[]{:S(2)}) collective-permute-start(bf16[128,512]{1,0:T(8,128)(2,1)S(1)} %bitcast.34), channel_id=1, source_target_pairs={{16,28},{20,24},{24,20},{28,16},{17,29},{21,25},{25,21},{29,17},{1... | collective-permute-start | bytes 393224 | tf_op jit(solution)/shard_map/ppermute | solution.py:93
  18.9 36.5 %collective-permute-start = (bf16[128,512]{1,0:T(8,128)(2,1)S(1)}, bf16[128,512]{1,0:T(8,128)(2,1)S(1)}, u32[]{:S(2)}, u32[]{:S(2)}) collective-permute-start(bf16[128,512]{1,0:T(8,128)(2,1)S(1)} %bitcast.35), channel_id=1, source_target_pairs={{0,16},{4,20},{8,24},{12,28},{1,17},{5,21},{9,25},{13,29},{2,18},{... | collective-permute-start | bytes 393224 | tf_op jit(solution)/shard_map/ppermute | solution.py:17
  28.6 26.7 %collective-permute-start.1 = (bf16[128,512]{1,0:T(8,128)(2,1)S(1)}, bf16[128,512]{1,0:T(8,128)(2,1)S(1)}, u32[]{:S(2)}, u32[]{:S(2)}) collective-permute-start(bf16[128,512]{1,0:T(8,128)(2,1)S(1)} %bitcast.36), channel_id=1, source_target_pairs={{0,12},{4,16},{8,20},{12,24},{16,28},{1,13},{5,17},{9,21},{13,25},... | collective-permute-start | bytes 393224 | tf_op jit(solution)/shard_map/ppermute | solution.py:17
  30.6 24.8 %collective-permute-start.2 = (bf16[128,512]{1,0:T(8,128)(2,1)S(1)}, bf16[128,512]{1,0:T(8,128)(2,1)S(1)}, u32[]{:S(2)}, u32[]{:S(2)}) collective-permute-start(bf16[128,512]{1,0:T(8,128)(2,1)S(1)} %bitcast.37), channel_id=1, source_target_pairs={{0,8},{4,12},{8,16},{12,20},{16,24},{20,28},{1,9},{5,13},{9,17},{1... | collective-permute-start | bytes 393224 | tf_op jit(solution)/shard_map/ppermute | solution.py:17
  32.4 7.8 %collective-permute-start.6 = (bf16[128,512]{1,0:T(8,128)(2,1)S(1)}, bf16[128,512]{1,0:T(8,128)(2,1)S(1)}, u32[]{:S(2)}, u32[]{:S(2)}) collective-permute-start(bf16[128,512]{1,0:T(8,128)(2,1)S(1)} %bitcast.50), channel_id=1, source_target_pairs={{12,0},{16,4},{20,8},{24,12},{28,16},{13,1},{17,5},{21,9},{25,13},... | collective-permute-start | bytes 393224 | tf_op jit(solution)/shard_map/ppermute | solution.py:17
  33.7 7.7 %collective-permute-start.7 = (bf16[128,512]{1,0:T(8,128)(2,1)S(1)}, bf16[128,512]{1,0:T(8,128)(2,1)S(1)}, u32[]{:S(2)}, u32[]{:S(2)}) collective-permute-start(bf16[128,512]{1,0:T(8,128)(2,1)S(1)} %bitcast.38), channel_id=1, source_target_pairs={{20,28},{28,20},{21,29},{29,21},{22,30},{30,22},{23,31},{31,23}} | collective-permute-start | bytes 393224 | tf_op jit(solution)/shard_map/ppermute | solution.py:93
  40.2 6.8 %collective-permute-start.8 = (bf16[128,512]{1,0:T(8,128)(2,1)S(1)}, bf16[128,512]{1,0:T(8,128)(2,1)S(1)}, u32[]{:S(2)}, u32[]{:S(2)}) collective-permute-start(bf16[128,512]{1,0:T(8,128)(2,1)S(1)} %bitcast.51), channel_id=1, source_target_pairs={{8,0},{12,4},{16,8},{20,12},{24,16},{28,20},{9,1},{13,5},{17,9},{2... | collective-permute-start | bytes 393224 | tf_op jit(solution)/shard_map/ppermute | solution.py:17
  41.5 12.5 %collective-permute-start.9 = (bf16[128,512]{1,0:T(8,128)(2,1)S(1)}, bf16[128,512]{1,0:T(8,128)(2,1)S(1)}, u32[]{:S(2)}, u32[]{:S(2)}) collective-permute-start(bf16[128,512]{1,0:T(8,128)(2,1)S(1)} %bitcast.40), channel_id=1, source_target_pairs={{24,28},{28,24},{25,29},{29,25},{26,30},{30,26},{27,31},{31,27}} | collective-permute-start | bytes 393224 | tf_op jit(solution)/shard_map/ppermute | solution.py:93
  47.0 10.8 %collective-permute-start.3 = (bf16[128,512]{1,0:T(8,128)(2,1)S(1)}, bf16[128,512]{1,0:T(8,128)(2,1)S(1)}, u32[]{:S(2)}, u32[]{:S(2)}) collective-permute-start(bf16[128,512]{1,0:T(8,128)(2,1)S(1)} %bitcast.42), channel_id=1, source_target_pairs={{0,4},{4,8},{8,12},{12,16},{16,20},{20,24},{24,28},{1,5},{5,9},{9,... | collective-permute-start | bytes 393224 | tf_op jit(solution)/shard_map/ppermute | solution.py:17
  54.0 6.9 %collective-permute-start.10 = (bf16[128,512]{1,0:T(8,128)(2,1)S(1)}, bf16[128,512]{1,0:T(8,128)(2,1)S(1)}, u32[]{:S(2)}, u32[]{:S(2)}) collective-permute-start(bf16[128,512]{1,0:T(8,128)(2,1)S(1)} %bitcast.52), channel_id=1, source_target_pairs={{4,0},{8,4},{12,8},{16,12},{20,16},{24,20},{28,24},{5,1},{9,5},{13... | collective-permute-start | bytes 393224 | tf_op jit(solution)/shard_map/ppermute | solution.py:17
  62.1 1.3 %copy-start = (bf16[64,4,4096]{2,0,1:T(8,128)(2,1)}, bf16[64,4,4096]{2,0,1:T(8,128)(2,1)S(1)}, u32[]{:S(2)}) copy-start(bf16[64,4,4096]{2,0,1:T(8,128)(2,1)S(1)} %all-to-all-done) | copy-start | bytes 6291460

commit v3 on v2

--- a/solution.py
+++ b/solution.py
@@ -29,31 +29,41 @@
 ):
     side = pl.program_id(0)
     block_id = blocks_ref[side]
-    row_pos = block_id * half_rows + lax.broadcasted_iota(jnp.int32, (half_rows, window), 0)
-    key_pos = block_id * half_rows - pad_rows + lax.broadcasted_iota(
-        jnp.int32, (half_rows, window), 1
-    )
-    row_start = start_ref[...]
-    allowed = (key_pos <= row_pos) & (key_pos >= row_start)
-    bias = jnp.where(allowed, 0.0, -jnp.inf).astype(jnp.float32)
+    needed = blocks_ref[2 + side]
     kt_buf[...] = k_ref[...].T
     scale = 1.0 / math.sqrt(DH)
+    row_start = start_ref[...]
 
-    def one_member(g, carry):
-        col = pl.multiple_of(g * DH, DH)
-        q_g = q_ref[:, pl.ds(col, DH)]
-        scores = jnp.dot(q_g, kt_buf[...], preferred_element_type=jnp.float32)
-        scores = scores * scale + bias
-        top = jnp.max(scores, axis=1, keepdims=True)
-        weights = jnp.exp(scores - top)
-        total = jnp.sum(weights, axis=1, keepdims=True)
-        mixed = jnp.dot(
-            weights.astype(jnp.bfloat16), v_ref[...], preferred_element_type=jnp.float32
+    def dense(span):
+        skip = window - span
+        row_pos = block_id * half_rows + lax.broadcasted_iota(jnp.int32, (half_rows, span), 0)
+        key_pos = block_id * half_rows - pad_rows + skip + lax.broadcasted_iota(
+            jnp.int32, (half_rows, span), 1
         )
-        out_ref[:, pl.ds(col, DH)] = (mixed / total).astype(out_ref.dtype)
-        return carry
+        allowed = (key_pos <= row_pos) & (key_pos >= row_start)
+        bias = jnp.where(allowed, 0.0, -jnp.inf).astype(jnp.float32)
 
-    lax.fori_loop(0, group_size, one_member, 0)
+        def one_member(g, carry):
+            col = pl.multiple_of(g * DH, DH)
+            q_g = q_ref[:, pl.ds(col, DH)]
+            scores = jnp.dot(q_g, kt_buf[:, skip:], preferred_element_type=jnp.float32)
+            scores = scores * scale + bias
+            top = jnp.max(scores, axis=1, keepdims=True)
+            weights = jnp.exp(scores - top)
+            total = jnp.sum(weights, axis=1, keepdims=True)
+            mixed = jnp.dot(
+                weights.astype(jnp.bfloat16), v_ref[skip:, :], preferred_element_type=jnp.float32
+            )
+            out_ref[:, pl.ds(col, DH)] = (mixed / total).astype(out_ref.dtype)
+            return carry
+
+        lax.fori_loop(0, group_size, one_member, 0)
+
+    for count in range(1, window // half_rows + 1):
+
+        @pl.when(needed == count)
+        def _(count=count):
+            dense(count * half_rows)
 
 
 def on_device(queries, key_rows, value_rows, doc_lengths):
@@ -105,6 +115,8 @@
     block_ids = jnp.stack([my_shard, 2 * shards - 1 - my_shard]).astype(jnp.int32)
     positions = block_ids[:, None] * half_rows + jnp.arange(half_rows, dtype=jnp.int32)[None, :]
     starts = doc_start(positions.reshape(-1), doc_ends, doc_lengths).astype(jnp.int32)
+    needed = 1 + jnp.clip((block_ids * half_rows - starts[::half_rows] + half_rows - 1) // half_rows, 0, lookback)
+    block_ids = jnp.concatenate([block_ids, needed.astype(jnp.int32)])
     starts = starts.reshape(2, half_rows, 1)
 
     kernel = functools.partial(

time: 128 us -> 124 us (0.969)
  Pallas kernels: 33 us -> 29.6 us
  other arithmetic: 3.11 us -> 4.48 us
    pallas_call x1, Pallas kernels: 33 us -> 29.6 us  [on_device(): pl.pallas_call(kernel, out_shape=jax.ShapeDtypeStruct(head_queries.shape,...]
  transfers between devices with their start and end apart: 13 -> 13, of which waited for: 5 -> 5; matrix products, arithmetic and copies ran while one was open for 5% -> 6% of each run, Pallas kernels for 0% -> 0%
where the time goes in v3:
time: 124 us
  starting transfers between devices  35.5 us (29%)
  Pallas kernels  29.6 us (24%)
  blocking collectives  29.3 us (24%)
  waiting for transfers between devices  17 us (14%)
  local copies, waits for them, and re-layouts  7.93 us (6%)
  other arithmetic  4.48 us (4%)
    pallas_call x1, Pallas kernels, on_device(): pl.pallas_call(kernel, out_shape=jax.ShapeDtypeStruct(head_queries.shape,...  29.6 us
    all_to_all x1, blocking collectives, on_device(): lax.all_to_all(merged, 'kvh', split_axis=0, concat_axis=1, tiled=True)  29.3 us
    ppermute x8, starting transfers between devices, shifted(): return lax.ppermute(block, axis, route)  25.6 us
    ppermute x8, waiting for transfers between devices, shifted(): return lax.ppermute(block, axis, route)  15.9 us
    all_to_all x1, starting transfers between devices, on_device(): lax.all_to_all(kv_local, 'kvh', split_axis=1, concat_axis=0, tiled=True)  4.24 us
    all_to_all x1, starting transfers between devices, on_device(): lax.all_to_all(queries, 'kvh', split_axis=1, concat_axis=0, tiled=True)  3.61 us
    all_to_all x1, local copies, waits for them, and re-layouts, on_device(): lax.all_to_all(queries, 'kvh', split_axis=1, concat_axis=0, tiled=True)  3.13 us
  transfers between devices with their start and end apart: 13, of which 5 were waited for; matrix products, arithmetic and copies ran while one was open for 6% of the time, Pallas kernels for 0%

profile of v3, /device:TPU:0, one launch (start us, length us, event | category | flops | bytes accessed | tf_op | source)
XLA Modules:
  0.0 124.0 jit_solution(3722994440364741789)
XLA Ops:
  0.0 1.0 copy_bitcast_fusion.1
  1.0 0.7 pad_maximum_fusion.1
  1.7 4.2 %all-to-all-start.1 = ((bf16[64,4,512]{2,0,1:T(8,128)(2,1)}), bf16[64,4,512]{2,0,1:T(8,128)(2,1)S(1)}, u32[]{:S(2)}, u32[]{:S(2)}) async-start(bf16[64,4,512]{2,0,1:T(8,128)(2,1)} %pad_maximum_fusion.1), calls=%async_computation.1 | async-start | bytes 524288 | tf_op jit(solution)/shard_map/all_to_all | solution.py:80
  5.9 0.1 add_multiply_fusion
  6.0 0.1 add_bitcast_fusion
  6.1 0.8 reduce-window.8
  6.9 0.7 select_reduce_fusion
  7.7 0.1 slice.15
  7.8 3.1 %copy.26 = bf16[8,4,8,4096]{3,2,0,1:T(8,128)(2,1)} copy(bf16[8,4,8,4096]{3,2,1,0:T(8,128)(2,1)} %bitcast.45) | data formatting | bytes 4194304 | tf_op jit(solution)/shard_map/all_to_all | solution.py:74
  10.9 1.1 all-to-all-done.1
  12.0 3.6 %all-to-all-start = ((bf16[64,4,4096]{2,0,1:T(8,128)(2,1)}), bf16[64,4,4096]{2,0,1:T(8,128)(2,1)S(1)}, u32[]{:S(2)}, u32[]{:S(2)}) async-start(bf16[64,4,4096]{2,0,1:T(8,128)(2,1)} %bitcast.30), calls=%async_computation | async-start | bytes 4194304 | tf_op jit(solution)/shard_map/all_to_all | solution.py:74
  15.6 1.3 %collective-permute-start.4 = (bf16[128,512]{1,0:T(8,128)(2,1)S(1)}, bf16[128,512]{1,0:T(8,128)(2,1)S(1)}, u32[]{:S(2)}, u32[]{:S(2)}) collective-permute-start(bf16[128,512]{1,0:T(8,128)(2,1)S(1)} %bitcast.49), channel_id=1, source_target_pairs={{16,0},{20,4},{24,8},{28,12},{17,1},{21,5},{25,9},{29,13},{18,2},{... | collective-permute-start | bytes 393224 | tf_op jit(solution)/shard_map/ppermute | solution.py:17
  16.9 0.7 collective-permute-start.5
  17.6 0.1 clamp_add_fusion
  17.7 0.8 copy.17.start_ref
  18.5 0.6 pad_add_fusion.blocks_ref
  19.1 9.8 %collective-permute-start = (bf16[128,512]{1,0:T(8,128)(2,1)S(1)}, bf16[128,512]{1,0:T(8,128)(2,1)S(1)}, u32[]{:S(2)}, u32[]{:S(2)}) collective-permute-start(bf16[128,512]{1,0:T(8,128)(2,1)S(1)} %bitcast.35), channel_id=1, source_target_pairs={{0,16},{4,20},{8,24},{12,28},{1,17},{5,21},{9,25},{13,29},{2,18},{... | collective-permute-start | bytes 393224 | tf_op jit(solution)/shard_map/ppermute | solution.py:17
  28.8 1.9 %collective-permute-start.1 = (bf16[128,512]{1,0:T(8,128)(2,1)S(1)}, bf16[128,512]{1,0:T(8,128)(2,1)S(1)}, u32[]{:S(2)}, u32[]{:S(2)}) collective-permute-start(bf16[128,512]{1,0:T(8,128)(2,1)S(1)} %bitcast.36), channel_id=1, source_target_pairs={{0,12},{4,16},{8,20},{12,24},{16,28},{1,13},{5,17},{9,21},{13,25},... | collective-permute-start | bytes 393224 | tf_op jit(solution)/shard_map/ppermute | solution.py:17
  30.8 1.8 %collective-permute-start.2 = (bf16[128,512]{1,0:T(8,128)(2,1)S(1)}, bf16[128,512]{1,0:T(8,128)(2,1)S(1)}, u32[]{:S(2)}, u32[]{:S(2)}) collective-permute-start(bf16[128,512]{1,0:T(8,128)(2,1)S(1)} %bitcast.37), channel_id=1, source_target_pairs={{0,8},{4,12},{8,16},{12,20},{16,24},{20,28},{1,9},{5,13},{9,17},{1... | collective-permute-start | bytes 393224 | tf_op jit(solution)/shard_map/ppermute | solution.py:17
  32.6 0.0 collective-permute-done.4
  32.6 1.3 %collective-permute-start.6 = (bf16[128,512]{1,0:T(8,128)(2,1)S(1)}, bf16[128,512]{1,0:T(8,128)(2,1)S(1)}, u32[]{:S(2)}, u32[]{:S(2)}) collective-permute-start(bf16[128,512]{1,0:T(8,128)(2,1)S(1)} %bitcast.50), channel_id=1, source_target_pairs={{12,0},{16,4},{20,8},{24,12},{28,16},{13,1},{17,5},{21,9},{25,13},... | collective-permute-start | bytes 393224 | tf_op jit(solution)/shard_map/ppermute | solution.py:17
  33.9 0.0 collective-permute-done.5
  33.9 0.7 collective-permute-start.7
  34.6 0.1 select_dynamic-update-slice_fusion.3
  34.7 5.7 %collective-permute-done.6 = bf16[128,512]{1,0:T(8,128)(2,1)S(1)} collective-permute-done((bf16[128,512]{1,0:T(8,128)(2,1)S(1)}, bf16[128,512]{1,0:T(8,128)(2,1)S(1)}, u32[]{:S(2)}, u32[]{:S(2)}) %collective-permute-start.6) | collective-permute-done | bytes 131104 | tf_op jit(solution)/shard_map/ppermute | solution.py:17
  40.4 1.3 %collective-permute-start.8 = (bf16[128,512]{1,0:T(8,128)(2,1)S(1)}, bf16[128,512]{1,0:T(8,128)(2,1)S(1)}, u32[]{:S(2)}, u32[]{:S(2)}) collective-permute-start(bf16[128,512]{1,0:T(8,128)(2,1)S(1)} %bitcast.51), channel_id=1, source_target_pairs={{8,0},{12,4},{16,8},{20,12},{24,16},{28,20},{9,1},{13,5},{17,9},{2... | collective-permute-start | bytes 393224 | tf_op jit(solution)/shard_map/ppermute | solution.py:17
  41.7 0.0 collective-permute-done.7
  41.7 0.7 collective-permute-start.9
  42.3 0.1 select_dynamic-update-slice_fusion.2
  42.4 4.8 %collective-permute-done.8 = bf16[128,512]{1,0:T(8,128)(2,1)S(1)} collective-permute-done((bf16[128,512]{1,0:T(8,128)(2,1)S(1)}, bf16[128,512]{1,0:T(8,128)(2,1)S(1)}, u32[]{:S(2)}, u32[]{:S(2)}) %collective-permute-start.8) | collective-permute-done | bytes 131104 | tf_op jit(solution)/shard_map/ppermute | solution.py:17
  47.2 6.9 %collective-permute-start.3 = (bf16[128,512]{1,0:T(8,128)(2,1)S(1)}, bf16[128,512]{1,0:T(8,128)(2,1)S(1)}, u32[]{:S(2)}, u32[]{:S(2)}) collective-permute-start(bf16[128,512]{1,0:T(8,128)(2,1)S(1)} %bitcast.42), channel_id=1, source_target_pairs={{0,4},{4,8},{8,12},{12,16},{16,20},{20,24},{24,28},{1,5},{5,9},{9,... | collective-permute-start | bytes 393224 | tf_op jit(solution)/shard_map/ppermute | solution.py:17
  54.2 0.0 collective-permute-done.9
  54.2 1.3 %collective-permute-start.10 = (bf16[128,512]{1,0:T(8,128)(2,1)S(1)}, bf16[128,512]{1,0:T(8,128)(2,1)S(1)}, u32[]{:S(2)}, u32[]{:S(2)}) collective-permute-start(bf16[128,512]{1,0:T(8,128)(2,1)S(1)} %bitcast.52), channel_id=1, source_target_pairs={{4,0},{8,4},{12,8},{16,12},{20,16},{24,20},{28,24},{5,1},{9,5},{13... | collective-permute-start | bytes 393224 | tf_op jit(solution)/shard_map/ppermute | solution.py:17
  55.5 0.1 select_dynamic-update-slice_fusion.1
  55.5 0.0 collective-permute-done
  55.6 0.0 collective-permute-done.1
  55.6 0.0 collective-permute-done.2
  55.6 2.4 %collective-permute-done.3 = bf16[128,512]{1,0:T(8,128)(2,1)S(1)} collective-permute-done((bf16[128,512]{1,0:T(8,128)(2,1)S(1)}, bf16[128,512]{1,0:T(8,128)(2,1)S(1)}, u32[]{:S(2)}, u32[]{:S(2)}) %collective-permute-start.3) | collective-permute-done | bytes 131104 | tf_op jit(solution)/shard_map/ppermute | solution.py:17
  58.1 3.0 %collective-permute-done.10 = bf16[128,512]{1,0:T(8,128)(2,1)S(1)} collective-permute-done((bf16[128,512]{1,0:T(8,128)(2,1)S(1)}, bf16[128,512]{1,0:T(8,128)(2,1)S(1)}, u32[]{:S(2)}, u32[]{:S(2)}) %collective-permute-start.10) | collective-permute-done | bytes 131104 | tf_op jit(solution)/shard_map/ppermute | solution.py:17
  61.1 1.2 pad_maximum_fusion.k_ref.v_ref
  62.3 0.0 all-to-all-done
  62.3 0.0 copy-start
  62.3 1.3 %copy-done = bf16[64,4,4096]{2,0,1:T(8,128)(2,1)} copy-done((bf16[64,4,4096]{2,0,1:T(8,128)(2,1)}, bf16[64,4,4096]{2,0,1:T(8,128)(2,1)S(1)}, u32[]{:S(2)}) %copy-start) | copy-done | bytes 2097176
  63.6 29.6 %shard_map.46 = bf16[256,4096]{1,0:T(8,128)(2,1)} custom-call(s32[4]{0:T(128)} %pad_add_fusion.blocks_ref, bf16[256,4096]{1,0:T(8,128)(2,1)} %bitcast.31, s32[2,128,1]{2,1,0:T(8,128)} %copy.17.start_ref, bf16[2,640,512]{2,1,0:T(8,128)(2,1)} %pad_maximum_fusion.k_ref.v_ref, bf16[2,640,512]{2,1,0:T(8,128)(2,1)} %pad_maximum_fusion.k_ref.v_ref), custom_call_target="tpu_custom_call" | custom-call | tf_op jit(solution)/shard_map/pallas_call | solution.py:130
  93.2 29.3 %all_to_all.53 = bf16[4,64,4096]{2,1,0:T(8,128)(2,1)S(1)} all-to-all(bf16[4,64,4096]{2,1,0:T(8,128)(2,1)} %bitcast.32), channel_id=1, replica_groups=mesh['seq'=8,'kvh'=4] {'kvh'}, dimensions={0} | all-to-all | bytes 4194304 | tf_op jit(solution)/shard_map/all_to_all | solution.py:148
  122.5 1.5 %copy.22 = bf16[4,8,8,4096]{3,2,0,1:T(8,128)(2,1)} copy(bf16[4,8,8,4096]{3,2,1,0:T(8,128)(2,1)S(1)} %bitcast.33) | data formatting | bytes 4194304 | tf_op jit(solution)/shard_map/all_to_all | solution.py:148
  (7 shorter events, 0.1 us)
Async XLA Ops:
  1.7 10.3 %all-to-all-start.1 = ((bf16[64,4,512]{2,0,1:T(8,128)(2,1)}), bf16[64,4,512]{2,0,1:T(8,128)(2,1)S(1)}, u32[]{:S(2)}, u32[]{:S(2)}) async-start(bf16[64,4,512]{2,0,1:T(8,128)(2,1)} %pad_maximum_fusion.1), calls=%async_computation.1 | async-start | bytes 524288 | tf_op jit(solution)/shard_map/all_to_all | solution.py:80
  12.0 50.3 %all-to-all-start = ((bf16[64,4,4096]{2,0,1:T(8,128)(2,1)}), bf16[64,4,4096]{2,0,1:T(8,128)(2,1)S(1)}, u32[]{:S(2)}, u32[]{:S(2)}) async-start(bf16[64,4,4096]{2,0,1:T(8,128)(2,1)} %bitcast.30), calls=%async_computation | async-start | bytes 4194304 | tf_op jit(solution)/shard_map/all_to_all | solution.py:74
  15.6 17.0 %collective-permute-start.4 = (bf16[128,512]{1,0:T(8,128)(2,1)S(1)}, bf16[128,512]{1,0:T(8,128)(2,1)S(1)}, u32[]{:S(2)}, u32[]{:S(2)}) collective-permute-start(bf16[128,512]{1,0:T(8,128)(2,1)S(1)} %bitcast.49), channel_id=1, source_target_pairs={{16,0},{20,4},{24,8},{28,12},{17,1},{21,5},{25,9},{29,13},{18,2},{... | collective-permute-start | bytes 393224 | tf_op jit(solution)/shard_map/ppermute | solution.py:17
  16.9 17.0 %collective-permute-start.5 = (bf16[128,512]{1,0:T(8,128)(2,1)S(1)}, bf16[128,512]{1,0:T(8,128)(2,1)S(1)}, u32[]{:S(2)}, u32[]{:S(2)}) collective-permute-start(bf16[128,512]{1,0:T(8,128)(2,1)S(1)} %bitcast.34), channel_id=1, source_target_pairs={{16,28},{20,24},{24,20},{28,16},{17,29},{21,25},{25,21},{29,17},{1... | collective-permute-start | bytes 393224 | tf_op jit(solution)/shard_map/ppermute | solution.py:103
  19.1 36.5 %collective-permute-start = (bf16[128,512]{1,0:T(8,128)(2,1)S(1)}, bf16[128,512]{1,0:T(8,128)(2,1)S(1)}, u32[]{:S(2)}, u32[]{:S(2)}) collective-permute-start(bf16[128,512]{1,0:T(8,128)(2,1)S(1)} %bitcast.35), channel_id=1, source_target_pairs={{0,16},{4,20},{8,24},{12,28},{1,17},{5,21},{9,25},{13,29},{2,18},{... | collective-permute-start | bytes 393224 | tf_op jit(solution)/shard_map/ppermute | solution.py:17
  28.8 26.7 %collective-permute-start.1 = (bf16[128,512]{1,0:T(8,128)(2,1)S(1)}, bf16[128,512]{1,0:T(8,128)(2,1)S(1)}, u32[]{:S(2)}, u32[]{:S(2)}) collective-permute-start(bf16[128,512]{1,0:T(8,128)(2,1)S(1)} %bitcast.36), channel_id=1, source_target_pairs={{0,12},{4,16},{8,20},{12,24},{16,28},{1,13},{5,17},{9,21},{13,25},... | collective-permute-start | bytes 393224 | tf_op jit(solution)/shard_map/ppermute | solution.py:17
  30.8 24.8 %collective-permute-start.2 = (bf16[128,512]{1,0:T(8,128)(2,1)S(1)}, bf16[128,512]{1,0:T(8,128)(2,1)S(1)}, u32[]{:S(2)}, u32[]{:S(2)}) collective-permute-start(bf16[128,512]{1,0:T(8,128)(2,1)S(1)} %bitcast.37), channel_id=1, source_target_pairs={{0,8},{4,12},{8,16},{12,20},{16,24},{20,28},{1,9},{5,13},{9,17},{1... | collective-permute-start | bytes 393224 | tf_op jit(solution)/shard_map/ppermute | solution.py:17
  32.6 7.8 %collective-permute-start.6 = (bf16[128,512]{1,0:T(8,128)(2,1)S(1)}, bf16[128,512]{1,0:T(8,128)(2,1)S(1)}, u32[]{:S(2)}, u32[]{:S(2)}) collective-permute-start(bf16[128,512]{1,0:T(8,128)(2,1)S(1)} %bitcast.50), channel_id=1, source_target_pairs={{12,0},{16,4},{20,8},{24,12},{28,16},{13,1},{17,5},{21,9},{25,13},... | collective-permute-start | bytes 393224 | tf_op jit(solution)/shard_map/ppermute | solution.py:17
  33.9 7.7 %collective-permute-start.7 = (bf16[128,512]{1,0:T(8,128)(2,1)S(1)}, bf16[128,512]{1,0:T(8,128)(2,1)S(1)}, u32[]{:S(2)}, u32[]{:S(2)}) collective-permute-start(bf16[128,512]{1,0:T(8,128)(2,1)S(1)} %bitcast.38), channel_id=1, source_target_pairs={{20,28},{28,20},{21,29},{29,21},{22,30},{30,22},{23,31},{31,23}} | collective-permute-start | bytes 393224 | tf_op jit(solution)/shard_map/ppermute | solution.py:103
  40.4 6.8 %collective-permute-start.8 = (bf16[128,512]{1,0:T(8,128)(2,1)S(1)}, bf16[128,512]{1,0:T(8,128)(2,1)S(1)}, u32[]{:S(2)}, u32[]{:S(2)}) collective-permute-start(bf16[128,512]{1,0:T(8,128)(2,1)S(1)} %bitcast.51), channel_id=1, source_target_pairs={{8,0},{12,4},{16,8},{20,12},{24,16},{28,20},{9,1},{13,5},{17,9},{2... | collective-permute-start | bytes 393224 | tf_op jit(solution)/shard_map/ppermute | solution.py:17
  41.7 12.5 %collective-permute-start.9 = (bf16[128,512]{1,0:T(8,128)(2,1)S(1)}, bf16[128,512]{1,0:T(8,128)(2,1)S(1)}, u32[]{:S(2)}, u32[]{:S(2)}) collective-permute-start(bf16[128,512]{1,0:T(8,128)(2,1)S(1)} %bitcast.40), channel_id=1, source_target_pairs={{24,28},{28,24},{25,29},{29,25},{26,30},{30,26},{27,31},{31,27}} | collective-permute-start | bytes 393224 | tf_op jit(solution)/shard_map/ppermute | solution.py:103
  47.2 10.8 %collective-permute-start.3 = (bf16[128,512]{1,0:T(8,128)(2,1)S(1)}, bf16[128,512]{1,0:T(8,128)(2,1)S(1)}, u32[]{:S(2)}, u32[]{:S(2)}) collective-permute-start(bf16[128,512]{1,0:T(8,128)(2,1)S(1)} %bitcast.42), channel_id=1, source_target_pairs={{0,4},{4,8},{8,12},{12,16},{16,20},{20,24},{24,28},{1,5},{5,9},{9,... | collective-permute-start | bytes 393224 | tf_op jit(solution)/shard_map/ppermute | solution.py:17
  54.2 6.9 %collective-permute-start.10 = (bf16[128,512]{1,0:T(8,128)(2,1)S(1)}, bf16[128,512]{1,0:T(8,128)(2,1)S(1)}, u32[]{:S(2)}, u32[]{:S(2)}) collective-permute-start(bf16[128,512]{1,0:T(8,128)(2,1)S(1)} %bitcast.52), channel_id=1, source_target_pairs={{4,0},{8,4},{12,8},{16,12},{20,16},{24,20},{28,24},{5,1},{9,5},{13... | collective-permute-start | bytes 393224 | tf_op jit(solution)/shard_map/ppermute | solution.py:17
  62.3 1.3 %copy-start = (bf16[64,4,4096]{2,0,1:T(8,128)(2,1)}, bf16[64,4,4096]{2,0,1:T(8,128)(2,1)S(1)}, u32[]{:S(2)}) copy-start(bf16[64,4,4096]{2,0,1:T(8,128)(2,1)S(1)} %all-to-all-done) | copy-start | bytes 6291460
